TPU v7x, 32 devices: a whole 2x2x4 slice. The times are simulated.
32 devices in a mesh: vol: 8 (over z, y), orient: 4 (over x, core).
Axes of the slice: x: 2, y: 2, z: 4, core: 2. Of those that a mesh axis runs over, the one named last changes fastest.
Arguments:
- tomogram: bfloat16 [640, 512, 256], P('vol', 'orient'), may hold values from -40 to 40
- templates: bfloat16 [4, 32, 1024], P('orient'), may hold values from 0 to 5
- corner_z: int32 [8, 60], P('vol', 'orient'), may hold values from 0 to 16
- corner_y: int32 [8, 60], P('vol', 'orient'), may hold values from 0 to 64
- corner_x: int32 [8, 60], P('vol', 'orient'), may hold values from 0 to 192
- loads: int32 [8, 4, 8], P('vol', 'orient'), may hold values from 0 to 2, as said below
Outputs:
- peaks: float32 [8, 60, 4], P('vol', 'orient')
- best: float32 [8, 60], P('vol', 'orient')
Inputs may be any that keep to these rules, and one draw needn't show every extreme that they name: `loads`: entry [v, o, m] is the number of candidates that owner (v, o) hands to matcher (m, o). Owner (v, o) holds as many candidates as its row sums to, at most 15, and in every orient column one owner holds exactly 15. Every matcher receives exactly 8 candidates. Some entry equals 2.
All inputs are finite; a program needn't handle non-finite values.
Results may differ from a plain program's by a relative error of at most 0.0064.
Values may be sent and summed in bfloat16 or wider, within the bound.
No kernel may reach another device: no remote copies, remote signals or barrier semaphores. Data moves between devices by JAX's collectives and lax.ppermute only.
A program may use at most 128 MiB of HBM per device.

v0:
```python
import math

import jax
import jax.numpy as jnp
from jax import lax
from jax.sharding import PartitionSpec as P

BOX = 64
TMPL = 32
SHIFT = 8
HALF = 33
LIVE = 8


epsilon = 1e-05


def product(pattern, operand_a, operand_b):
    return jnp.einsum(pattern, operand_a, operand_b, precision=lax.Precision.HIGHEST)


def lower_product(pattern, operand_a, operand_b):
    return jnp.einsum(
        pattern,
        operand_a.astype(jnp.bfloat16),
        operand_b.astype(jnp.bfloat16),
        preferred_element_type=jnp.float32,
    )


def shift_anchor():
    return (BOX - TMPL) // 2 - SHIFT // 2


def phases(count_out, count_in, offset):
    out_index = jnp.arange(count_out, dtype=jnp.int32) + offset
    in_index = jnp.arange(count_in, dtype=jnp.int32)
    turn_index = out_index[:, None] * in_index[None, :] % BOX
    phase_angle = turn_index.astype(jnp.float32) * (2.0 * math.pi / BOX)
    return (jnp.cos(phase_angle), jnp.sin(phase_angle))


def forward(volume):
    length = volume.shape[0]
    cos_full, sin_full = phases(BOX, length, 0)
    cos_half, sin_half = phases(HALF, length, 0)
    real_a = lower_product("abx,kx->abk", volume, cos_full)
    imag_a = -lower_product("abx,kx->abk", volume, sin_full)
    real_b = lower_product("ayk,jy->ajk", real_a, cos_full) + lower_product(
        "ayk,jy->ajk", imag_a, sin_full
    )
    imag_b = lower_product("ayk,jy->ajk", imag_a, cos_full) - lower_product(
        "ayk,jy->ajk", real_a, sin_full
    )
    real_c = lower_product("xjk,hx->hjk", real_b, cos_half) + lower_product(
        "xjk,hx->hjk", imag_b, sin_half
    )
    imag_c = lower_product("xjk,hx->hjk", imag_b, cos_half) - lower_product(
        "xjk,hx->hjk", real_b, sin_half
    )
    return jnp.stack([real_c, imag_c])


def template_spectrum(flat_cube):
    volume = flat_cube.astype(jnp.float32).reshape(TMPL, TMPL, TMPL)
    centred = volume - jnp.mean(volume)
    unit_cube = centred / jnp.sqrt(jnp.mean(centred * centred) + epsilon)
    return forward(unit_cube).astype(jnp.bfloat16)


def band_table():
    lower_edge = jnp.arange(SHIFT, dtype=jnp.int32)[:, None] + shift_anchor()
    cell_index = jnp.arange(BOX, dtype=jnp.int32)[None, :]
    return ((cell_index >= lower_edge) & (cell_index < lower_edge + TMPL)).astype(jnp.float32)


def window_rms(volume):
    window_band = band_table()
    squares = volume * volume
    sums_a = product("abc,sa->sbc", squares, window_band)
    sums_b = product("sbc,tb->stc", sums_a, window_band)
    sums_c = product("stc,uc->stu", sums_b, window_band)
    return jnp.sqrt(sums_c / float(TMPL**3) + epsilon)


def peaks_of(box_spectra, box_rms, spectrum):
    real_t = spectrum[0].astype(jnp.float32)
    imag_t = spectrum[1].astype(jnp.float32)
    real_v = box_spectra[:, 0]
    imag_v = box_spectra[:, 1]
    real_p = real_t * real_v + imag_t * imag_v
    imag_p = real_t * imag_v - imag_t * real_v
    cos_first, sin_first = phases(SHIFT, HALF, shift_anchor())
    freq_index = jnp.arange(HALF, dtype=jnp.int32)
    weight = jnp.where(freq_index % (BOX // 2) == 0, 1.0, 2.0) / float(BOX**3)
    cos_first = cos_first * weight[None, :]
    sin_first = sin_first * weight[None, :]
    real_g = lower_product("chjk,sh->csjk", real_p, cos_first) - lower_product(
        "chjk,sh->csjk", imag_p, sin_first
    )
    imag_g = lower_product("chjk,sh->csjk", imag_p, cos_first) + lower_product(
        "chjk,sh->csjk", real_p, sin_first
    )
    cos_rest, sin_rest = phases(SHIFT, BOX, shift_anchor())
    real_h = lower_product("csjk,tj->cstk", real_g, cos_rest) - lower_product(
        "csjk,tj->cstk", imag_g, sin_rest
    )
    imag_h = lower_product("csjk,tj->cstk", imag_g, cos_rest) + lower_product(
        "csjk,tj->cstk", real_g, sin_rest
    )
    correlation = lower_product("cstk,uk->cstu", real_h, cos_rest) - lower_product(
        "cstk,uk->cstu", imag_h, sin_rest
    )
    scores = correlation / (box_rms * math.sqrt(float(TMPL**3)))
    return jnp.max(scores, axis=(1, 2, 3))


def extract(block, along_z, along_y, along_x):

    def extract_single(corner_a, corner_b, corner_c):
        return lax.dynamic_slice(block, (corner_a, corner_b, corner_c), (BOX, BOX, BOX)).reshape(
            BOX, BOX * BOX
        )

    return jax.vmap(extract_single)(along_z, along_y, along_x)


def candidates(box_rows):

    def candidates_single(flat_box):
        volume = flat_box.astype(jnp.float32).reshape(BOX, BOX, BOX)
        return (forward(volume), window_rms(volume))

    return lax.map(candidates_single, box_rows)


def match_all(box_spectra, box_rms, templates):
    values = lax.map(
        lambda flat_cube: peaks_of(box_spectra, box_rms, template_spectrum(flat_cube)),
        lax.all_gather(templates, "orient", axis=0, tiled=True),
    )
    return values.T


def per_device(tomogram, templates, corner_z, corner_y, corner_x, loads):
    vol_count = lax.axis_size("vol")
    own_total = corner_z.shape[1]
    capacity = (own_total + vol_count - 1) // vol_count
    orient_total = templates.shape[0] * lax.axis_size("orient")
    load_row = loads[0, 0]
    starts_at = jnp.cumsum(load_row) - load_row
    own_slots = jnp.arange(own_total, dtype=jnp.int32)
    sub_slot = jnp.arange(capacity, dtype=jnp.int32)
    box_rows = extract(tomogram, corner_z[0], corner_y[0], corner_x[0])
    chosen = (own_slots[None, None, :] == starts_at[:, None, None] + sub_slot[None, :, None]) & (
        sub_slot[None, :, None] < load_row[:, None, None]
    )
    picker = chosen.reshape(vol_count * capacity, own_total)
    outgoing = jnp.einsum(
        "rj,jz->rz",
        picker.astype(jnp.bfloat16),
        box_rows.reshape(own_total, BOX**3),
        preferred_element_type=jnp.float32,
    ).astype(jnp.bfloat16)
    live_flags = (sub_slot[None, :] < load_row[:, None]).astype(jnp.bfloat16)
    arrived, arrived_flags = (
        lax.all_to_all(
            outgoing.reshape(vol_count, capacity, BOX**3),
            "vol",
            split_axis=0,
            concat_axis=0,
            tiled=True,
        ),
        lax.all_to_all(live_flags, "vol", split_axis=0, concat_axis=0, tiled=True),
    )
    flag_ints = (arrived_flags.reshape(vol_count * capacity) > 0.5).astype(jnp.int32)
    arrive_rank = jnp.cumsum(flag_ints) - flag_ints
    live_slots = jnp.arange(LIVE, dtype=jnp.int32)
    gather_rows = (arrive_rank[None, :] == live_slots[:, None]) & (flag_ints[None, :] > 0)
    compact = jnp.einsum(
        "lr,rz->lz",
        gather_rows.astype(jnp.bfloat16),
        arrived.reshape(vol_count * capacity, BOX**3),
        preferred_element_type=jnp.float32,
    ).astype(jnp.bfloat16)
    box_spectra, box_rms = candidates(compact.reshape(LIVE, BOX, BOX * BOX))
    results = match_all(box_spectra, box_rms, templates)
    sent_back = product("lr,lo->ro", gather_rows.astype(jnp.float32), results)
    returned = lax.all_to_all(
        sent_back.reshape(vol_count, capacity, orient_total),
        "vol",
        split_axis=0,
        concat_axis=0,
        tiled=True,
    )
    matched = product("mqj,mqo->jo", chosen.astype(jnp.float32), returned)
    return (matched[None], jnp.max(matched, axis=1)[None])


def solution(mesh):
    return jax.shard_map(
        per_device,
        mesh=mesh,
        in_specs=(
            P("vol", "orient", None),
            P("orient", None, None),
            P("vol", "orient"),
            P("vol", "orient"),
            P("vol", "orient"),
            P("vol", "orient", None),
        ),
        out_specs=(P("vol", "orient", None), P("vol", "orient")),
        check_vma=False,
    )
```

profile of v0, /device:TPU:0, one launch (start us, length us, event | category | flops | bytes accessed | tf_op | source)
XLA Modules:
  0.0 562.9 jit_solution(16152040857656057013)
XLA Ops:
  2.0 7.3 %all-to-all-start = ((bf16[8,1,2]{2,1,0:T(2,128)(2,1)}), bf16[8,1,2]{2,1,0:T(2,128)(2,1)S(1)}, u32[]{:S(2)}, u32[]{:S(2)}) async-start(bf16[8,1,2]{2,1,0:T(2,128)(2,1)} %compare_convert_fusion.1), calls=%async_computation | async-start | bytes 8192 | tf_op jit(solution)/shard_map/all_to_all | solution.py:174
  13.1 97.7 %while.30 = (s32[]{:T(128)}, bf16[80,128,256]{2,1,0:T(8,128)(2,1)}, s32[15,3]{0,1:T(4,128)S(1)}, bf16[15,64,64,64]{3,2,1,0:T(8,128)(2,1)}, s32[]{:T(128)}) while((s32[]{:T(128)}, bf16[80,128,256]{2,1,0:T(8,128)(2,1)}, s32[15,3]{0,1:T(4,128)S(1)}, bf16[15,64,64,64]{3,2,1,0:T(8,128)(2,1)}, s32[]{:T(128)}) %tuple.83), condition=%wide.while_cond, body=%wide.while_body.sunk | while | flops 2 | bytes 2098813 | solution.py:121
  13.8 5.9 %bitcast_dynamic-update-slice_fusion.2 = bf16[15,64,64,64]{3,2,1,0:T(8,128)(2,1)} fusion(bf16[15,64,64,64]{3,2,1,0:T(8,128)(2,1)} %get-tuple-element.323, s32[]{:T(128)S(6)} %copy.134, bf16[80,128,256]{2,1,0:T(8,128)(2,1)} %get-tuple-element.326, s32[]{:T(128)} %bitcast.305, s32[]{:T(128)} %bitcast.306, s32[]{:T(128)} %bitcast.307), kind=kLoop, calls=%fused_computation.296.clone.1 | loop fusion | bytes 2098692 | tf_op jit(solution)/shard_map/vmap()/gather
  20.3 5.9 %bitcast_dynamic-update-slice_fusion.2 = bf16[15,64,64,64]{3,2,1,0:T(8,128)(2,1)} fusion(bf16[15,64,64,64]{3,2,1,0:T(8,128)(2,1)} %get-tuple-element.323, s32[]{:T(128)S(6)} %copy.134, bf16[80,128,256]{2,1,0:T(8,128)(2,1)} %get-tuple-element.326, s32[]{:T(128)} %bitcast.305, s32[]{:T(128)} %bitcast.306, s32[]{:T(128)} %bitcast.307), kind=kLoop, calls=%fused_computation.296.clone.1 | loop fusion | bytes 2098692 | tf_op jit(solution)/shard_map/vmap()/gather
  26.9 5.9 %bitcast_dynamic-update-slice_fusion.2 = bf16[15,64,64,64]{3,2,1,0:T(8,128)(2,1)} fusion(bf16[15,64,64,64]{3,2,1,0:T(8,128)(2,1)} %get-tuple-element.323, s32[]{:T(128)S(6)} %copy.134, bf16[80,128,256]{2,1,0:T(8,128)(2,1)} %get-tuple-element.326, s32[]{:T(128)} %bitcast.305, s32[]{:T(128)} %bitcast.306, s32[]{:T(128)} %bitcast.307), kind=kLoop, calls=%fused_computation.296.clone.1 | loop fusion | bytes 2098692 | tf_op jit(solution)/shard_map/vmap()/gather
  33.4 5.9 %bitcast_dynamic-update-slice_fusion.2 = bf16[15,64,64,64]{3,2,1,0:T(8,128)(2,1)} fusion(bf16[15,64,64,64]{3,2,1,0:T(8,128)(2,1)} %get-tuple-element.323, s32[]{:T(128)S(6)} %copy.134, bf16[80,128,256]{2,1,0:T(8,128)(2,1)} %get-tuple-element.326, s32[]{:T(128)} %bitcast.305, s32[]{:T(128)} %bitcast.306, s32[]{:T(128)} %bitcast.307), kind=kLoop, calls=%fused_computation.296.clone.1 | loop fusion | bytes 2098692 | tf_op jit(solution)/shard_map/vmap()/gather
  39.9 5.9 %bitcast_dynamic-update-slice_fusion.2 = bf16[15,64,64,64]{3,2,1,0:T(8,128)(2,1)} fusion(bf16[15,64,64,64]{3,2,1,0:T(8,128)(2,1)} %get-tuple-element.323, s32[]{:T(128)S(6)} %copy.134, bf16[80,128,256]{2,1,0:T(8,128)(2,1)} %get-tuple-element.326, s32[]{:T(128)} %bitcast.305, s32[]{:T(128)} %bitcast.306, s32[]{:T(128)} %bitcast.307), kind=kLoop, calls=%fused_computation.296.clone.1 | loop fusion | bytes 2098692 | tf_op jit(solution)/shard_map/vmap()/gather
  46.4 5.9 %bitcast_dynamic-update-slice_fusion.2 = bf16[15,64,64,64]{3,2,1,0:T(8,128)(2,1)} fusion(bf16[15,64,64,64]{3,2,1,0:T(8,128)(2,1)} %get-tuple-element.323, s32[]{:T(128)S(6)} %copy.134, bf16[80,128,256]{2,1,0:T(8,128)(2,1)} %get-tuple-element.326, s32[]{:T(128)} %bitcast.305, s32[]{:T(128)} %bitcast.306, s32[]{:T(128)} %bitcast.307), kind=kLoop, calls=%fused_computation.296.clone.1 | loop fusion | bytes 2098692 | tf_op jit(solution)/shard_map/vmap()/gather
  53.0 5.9 %bitcast_dynamic-update-slice_fusion.2 = bf16[15,64,64,64]{3,2,1,0:T(8,128)(2,1)} fusion(bf16[15,64,64,64]{3,2,1,0:T(8,128)(2,1)} %get-tuple-element.323, s32[]{:T(128)S(6)} %copy.134, bf16[80,128,256]{2,1,0:T(8,128)(2,1)} %get-tuple-element.326, s32[]{:T(128)} %bitcast.305, s32[]{:T(128)} %bitcast.306, s32[]{:T(128)} %bitcast.307), kind=kLoop, calls=%fused_computation.296.clone.1 | loop fusion | bytes 2098692 | tf_op jit(solution)/shard_map/vmap()/gather
  59.5 5.9 %bitcast_dynamic-update-slice_fusion.2 = bf16[15,64,64,64]{3,2,1,0:T(8,128)(2,1)} fusion(bf16[15,64,64,64]{3,2,1,0:T(8,128)(2,1)} %get-tuple-element.323, s32[]{:T(128)S(6)} %copy.134, bf16[80,128,256]{2,1,0:T(8,128)(2,1)} %get-tuple-element.326, s32[]{:T(128)} %bitcast.305, s32[]{:T(128)} %bitcast.306, s32[]{:T(128)} %bitcast.307), kind=kLoop, calls=%fused_computation.296.clone.1 | loop fusion | bytes 2098692 | tf_op jit(solution)/shard_map/vmap()/gather
  66.1 5.9 %bitcast_dynamic-update-slice_fusion.2 = bf16[15,64,64,64]{3,2,1,0:T(8,128)(2,1)} fusion(bf16[15,64,64,64]{3,2,1,0:T(8,128)(2,1)} %get-tuple-element.323, s32[]{:T(128)S(6)} %copy.134, bf16[80,128,256]{2,1,0:T(8,128)(2,1)} %get-tuple-element.326, s32[]{:T(128)} %bitcast.305, s32[]{:T(128)} %bitcast.306, s32[]{:T(128)} %bitcast.307), kind=kLoop, calls=%fused_computation.296.clone.1 | loop fusion | bytes 2098692 | tf_op jit(solution)/shard_map/vmap()/gather
  72.7 5.9 %bitcast_dynamic-update-slice_fusion.2 = bf16[15,64,64,64]{3,2,1,0:T(8,128)(2,1)} fusion(bf16[15,64,64,64]{3,2,1,0:T(8,128)(2,1)} %get-tuple-element.323, s32[]{:T(128)S(6)} %copy.134, bf16[80,128,256]{2,1,0:T(8,128)(2,1)} %get-tuple-element.326, s32[]{:T(128)} %bitcast.305, s32[]{:T(128)} %bitcast.306, s32[]{:T(128)} %bitcast.307), kind=kLoop, calls=%fused_computation.296.clone.1 | loop fusion | bytes 2098692 | tf_op jit(solution)/shard_map/vmap()/gather
  79.2 5.5 bitcast_dynamic-update-slice_fusion.2
  85.3 5.8 %bitcast_dynamic-update-slice_fusion.2 = bf16[15,64,64,64]{3,2,1,0:T(8,128)(2,1)} fusion(bf16[15,64,64,64]{3,2,1,0:T(8,128)(2,1)} %get-tuple-element.323, s32[]{:T(128)S(6)} %copy.134, bf16[80,128,256]{2,1,0:T(8,128)(2,1)} %get-tuple-element.326, s32[]{:T(128)} %bitcast.305, s32[]{:T(128)} %bitcast.306, s32[]{:T(128)} %bitcast.307), kind=kLoop, calls=%fused_computation.296.clone.1 | loop fusion | bytes 2098692 | tf_op jit(solution)/shard_map/vmap()/gather
  91.8 5.9 %bitcast_dynamic-update-slice_fusion.2 = bf16[15,64,64,64]{3,2,1,0:T(8,128)(2,1)} fusion(bf16[15,64,64,64]{3,2,1,0:T(8,128)(2,1)} %get-tuple-element.323, s32[]{:T(128)S(6)} %copy.134, bf16[80,128,256]{2,1,0:T(8,128)(2,1)} %get-tuple-element.326, s32[]{:T(128)} %bitcast.305, s32[]{:T(128)} %bitcast.306, s32[]{:T(128)} %bitcast.307), kind=kLoop, calls=%fused_computation.296.clone.1 | loop fusion | bytes 2098692 | tf_op jit(solution)/shard_map/vmap()/gather
  98.4 5.8 %bitcast_dynamic-update-slice_fusion.2 = bf16[15,64,64,64]{3,2,1,0:T(8,128)(2,1)} fusion(bf16[15,64,64,64]{3,2,1,0:T(8,128)(2,1)} %get-tuple-element.323, s32[]{:T(128)S(6)} %copy.134, bf16[80,128,256]{2,1,0:T(8,128)(2,1)} %get-tuple-element.326, s32[]{:T(128)} %bitcast.305, s32[]{:T(128)} %bitcast.306, s32[]{:T(128)} %bitcast.307), kind=kLoop, calls=%fused_computation.296.clone.1 | loop fusion | bytes 2098692 | tf_op jit(solution)/shard_map/vmap()/gather
  104.9 5.9 %bitcast_dynamic-update-slice_fusion.2 = bf16[15,64,64,64]{3,2,1,0:T(8,128)(2,1)} fusion(bf16[15,64,64,64]{3,2,1,0:T(8,128)(2,1)} %get-tuple-element.323, s32[]{:T(128)S(6)} %copy.134, bf16[80,128,256]{2,1,0:T(8,128)(2,1)} %get-tuple-element.326, s32[]{:T(128)} %bitcast.305, s32[]{:T(128)} %bitcast.306, s32[]{:T(128)} %bitcast.307), kind=kLoop, calls=%fused_computation.296.clone.1 | loop fusion | bytes 2098692 | tf_op jit(solution)/shard_map/vmap()/gather
  110.8 22.8 %reshape.351 = bf16[15,262144]{1,0:T(8,128)(2,1)} reshape(bf16[15,64,64,64]{3,2,1,0:T(8,128)(2,1)} %get-tuple-element.155) | data formatting | bytes 15728640 | tf_op jit(solution)/shard_map/reshape;vmap()/reshape | solution.py:162
  133.6 9.0 %convolution_convert_fusion.2 = bf16[16,262144]{1,0:T(8,128)(2,1)} fusion(bf16[15,262144]{1,0:T(8,128)(2,1)} %reshape.351, s32[16]{0:T(128)S(1)} %add.327, pred[16]{0:T(512)(128)(4,1)S(1)} %lt.208), kind=kOutput, calls=%fused_computation.298 | convolution fusion | flops 130023904 | bytes 16253008 | tf_op jit(solution)/shard_map/rj,jz->rz/dot_general | solution.py:159
  142.5 9.5 %reshape.352 = bf16[8,2,262144]{2,1,0:T(2,128)(2,1)} reshape(bf16[16,262144]{1,0:T(8,128)(2,1)} %convolution_convert_fusion.2) | data formatting | bytes 16777216 | tf_op jit(solution)/shard_map/reshape | solution.py:168
  152.0 5.2 all-to-all-start.1
  157.2 5.8 %all_gather.3 = bf16[4,32,1024]{2,1,0:T(8,128)(2,1)S(1)} all-gather(bf16[1,32,1024]{2,1,0:T(8,128)(2,1)S(1)} %copy-done), channel_id=1, replica_groups=mesh['vol'=8,'orient'=4] {'orient'}, dimensions={0}, use_global_device_ids=true | all-gather | bytes 327680 | tf_op jit(solution)/shard_map/all_gather | solution.py:140
  163.4 175.7 %all-to-all-done.1 = bf16[8,2,262144]{2,1,0:T(2,128)(2,1)} async-done(((bf16[8,2,262144]{2,1,0:T(2,128)(2,1)}), bf16[8,2,262144]{2,1,0:T(2,128)(2,1)}, u32[]{:S(2)}, u32[]{:S(2)}) %all-to-all-start.1) | async-done | bytes 8388640 | tf_op jit(solution)/shard_map/all_to_all | solution.py:167
  339.1 7.3 %reshape.353 = bf16[16,262144]{1,0:T(8,128)(2,1)} reshape(bf16[8,2,262144]{2,1,0:T(2,128)(2,1)} %all-to-all-done.1) | data formatting | bytes 16777216 | tf_op jit(solution)/shard_map/reshape | solution.py:183
  346.4 4.6 convolution_convert_fusion.3
  351.0 4.3 copy.55
  355.3 107.6 %while.28 = (s32[]{:T(128)}, f32[8,2,33,64,64]{4,2,3,0,1:T(8,128)}, f32[8,8,8,8]{3,2,1,0:T(8,128)S(1)}, bf16[8,64,4096]{2,1,0:T(8,128)(2,1)}, s32[]{:T(128)}) while((s32[]{:T(128)}, f32[8,2,33,64,64]{4,2,3,0,1:T(8,128)}, f32[8,8,8,8]{3,2,1,0:T(8,128)S(1)}, bf16[8,64,4096]{2,1,0:T(8,128)(2,1)}, s32[]{:T(128)}) %tuple.86), condition=%wide.region_3.4_spmd, body=%wide.region_2.3_spmd.sunk | while | flops 302638336 | bytes 23545104 | solution.py:134
  359.1 2.0 fusion.448
  367.2 1.7 fusion.447
  372.5 2.0 fusion.448
  380.6 1.7 fusion.447
  386.0 2.0 fusion.448
  394.1 1.7 fusion.447
  399.4 2.0 fusion.448
  412.7 2.0 fusion.448
  426.1 2.0 fusion.448
  434.3 1.7 fusion.447
  439.6 2.0 fusion.448
  447.7 1.8 fusion.447
  453.1 2.0 fusion.448
  461.2 1.7 fusion.447
  462.9 87.3 %while.29 = (s32[]{:T(128)}, f32[4,8]{1,0:T(4,128)S(1)}, bf16[4,32,1024]{2,1,0:T(8,128)(2,1)S(1)}, f32[8,2,33,64,64]{4,2,3,0,1:T(8,128)}, f32[8,8,8,8]{3,2,1,0:T...) while((s32[]{:T(128)}, f32[4,8]{1,0:T(4,128)S(1)}, bf16[4,32,1024]{2,1,0:T(8,128)(2,1)S(1)}, ...), condition=%wide.region_8.9_spmd, body=%wide.region_4.8_spmd.sunk | while | flops 175595168 | bytes 38847688 | solution.py:138
  470.3 8.3 %fusion.499 = (bf16[8,33,64,64]{3,1,2,0:T(8,128)(2,1)S(1)}, bf16[8,33,64,64]{3,1,2,0:T(8,128)(2,1)S(1)}) fusion(f32[8,2,33,64,64]{4,2,3,0,1:T(8,128)} %get-tuple-element.366, f32[33,64,64]{2,0,1:T(8,128)S(1)} %fusion.496, f32[33,64,64]{2,0,1:T(8,128)S(1)} %fusion.498), kind=kLoop, calls=%fused_computation.114.clone.1 | loop fusion | flops 8650752 | bytes 14057472 | tf_op jit(solution)/shard_map/while/body/eval_jaxpr/convert_element_type | solution.py:25
  492.1 8.3 %fusion.499 = (bf16[8,33,64,64]{3,1,2,0:T(8,128)(2,1)S(1)}, bf16[8,33,64,64]{3,1,2,0:T(8,128)(2,1)S(1)}) fusion(f32[8,2,33,64,64]{4,2,3,0,1:T(8,128)} %get-tuple-element.366, f32[33,64,64]{2,0,1:T(8,128)S(1)} %fusion.496, f32[33,64,64]{2,0,1:T(8,128)S(1)} %fusion.498), kind=kLoop, calls=%fused_computation.114.clone.1 | loop fusion | flops 8650752 | bytes 14057472 | tf_op jit(solution)/shard_map/while/body/eval_jaxpr/convert_element_type | solution.py:25
  513.9 8.3 %fusion.499 = (bf16[8,33,64,64]{3,1,2,0:T(8,128)(2,1)S(1)}, bf16[8,33,64,64]{3,1,2,0:T(8,128)(2,1)S(1)}) fusion(f32[8,2,33,64,64]{4,2,3,0,1:T(8,128)} %get-tuple-element.366, f32[33,64,64]{2,0,1:T(8,128)S(1)} %fusion.496, f32[33,64,64]{2,0,1:T(8,128)S(1)} %fusion.498), kind=kLoop, calls=%fused_computation.114.clone.1 | loop fusion | flops 8650752 | bytes 14057472 | tf_op jit(solution)/shard_map/while/body/eval_jaxpr/convert_element_type | solution.py:25
  535.6 8.3 %fusion.499 = (bf16[8,33,64,64]{3,1,2,0:T(8,128)(2,1)S(1)}, bf16[8,33,64,64]{3,1,2,0:T(8,128)(2,1)S(1)}) fusion(f32[8,2,33,64,64]{4,2,3,0,1:T(8,128)} %get-tuple-element.366, f32[33,64,64]{2,0,1:T(8,128)S(1)} %fusion.496, f32[33,64,64]{2,0,1:T(8,128)S(1)} %fusion.498), kind=kLoop, calls=%fused_computation.114.clone.1 | loop fusion | flops 8650752 | bytes 14057472 | tf_op jit(solution)/shard_map/while/body/eval_jaxpr/convert_element_type | solution.py:25
  551.0 3.6 all-to-all-start.2
  554.8 6.3 %all-to-all-done.2 = f32[8,2,4]{2,1,0:T(2,128)S(1)} async-done(((f32[8,2,4]{2,1,0:T(2,128)}), f32[8,2,4]{2,1,0:T(2,128)S(1)}, u32[]{:S(2)}, u32[]{:S(2)}) %all-to-all-start.2) | async-done | bytes 288 | tf_op jit(solution)/shard_map/all_to_all | solution.py:189
  (305 shorter events, 146.5 us)
Async XLA Ops:
  2.0 150.1 %all-to-all-start = ((bf16[8,1,2]{2,1,0:T(2,128)(2,1)}), bf16[8,1,2]{2,1,0:T(2,128)(2,1)S(1)}, u32[]{:S(2)}, u32[]{:S(2)}) async-start(bf16[8,1,2]{2,1,0:T(2,128)(2,1)} %compare_convert_fusion.1), calls=%async_computation | async-start | bytes 8192 | tf_op jit(solution)/shard_map/all_to_all | solution.py:174
  10.0 2.2 copy-start.7
  12.3 0.8 copy-start.1
  152.0 5.2 copy-start
  152.0 187.0 %all-to-all-start.1 = ((bf16[8,2,262144]{2,1,0:T(2,128)(2,1)}), bf16[8,2,262144]{2,1,0:T(2,128)(2,1)}, u32[]{:S(2)}, u32[]{:S(2)}) async-start(bf16[8,2,262144]{2,1,0:T(2,128)(2,1)} %reshape.352), calls=%async_computation.1 | async-start | bytes 16777216 | tf_op jit(solution)/shard_map/all_to_all | solution.py:167
  163.3 183.1 %copy-start.3 = (s32[16]{0:T(128)}, s32[16]{0:T(128)S(1)}, u32[]{:S(2)}) copy-start(s32[16]{0:T(128)S(1)} %sub.93) | copy-start | bytes 196
  163.4 183.0 %copy-start.5 = (pred[16]{0:T(512)(128)(4,1)}, pred[16]{0:T(512)(128)(4,1)S(1)}, u32[]{:S(2)}) copy-start(pred[16]{0:T(512)(128)(4,1)S(1)} %broadcast_compare_fusion) | copy-start | bytes 52
  462.9 87.3 %copy-start.4 = (s32[16]{0:T(128)S(1)}, s32[16]{0:T(128)}, u32[]{:S(2)}) copy-start(s32[16]{0:T(128)} %copy-done.3) | copy-start | bytes 196
  462.9 87.3 %copy-start.6 = (pred[16]{0:T(512)(128)(4,1)S(1)}, pred[16]{0:T(512)(128)(4,1)}, u32[]{:S(2)}) copy-start(pred[16]{0:T(512)(128)(4,1)} %copy-done.5) | copy-start | bytes 52
  462.9 91.8 %copy-start.8 = (pred[8,2]{1,0:T(8,128)(4,1)S(1)}, pred[8,2]{1,0:T(8,128)(4,1)}, u32[]{:S(2)}) copy-start(pred[8,2]{1,0:T(8,128)(4,1)} %copy-done.7) | copy-start | bytes 52
  462.9 91.9 %copy-start.2 = (s32[8,2]{1,0:T(8,128)S(1)}, s32[8,2]{1,0:T(8,128)}, u32[]{:S(2)}) copy-start(s32[8,2]{1,0:T(8,128)} %copy-done.1) | copy-start | bytes 196
  551.0 10.2 %all-to-all-start.2 = ((f32[8,2,4]{2,1,0:T(2,128)}), f32[8,2,4]{2,1,0:T(2,128)S(1)}, u32[]{:S(2)}, u32[]{:S(2)}) async-start(f32[8,2,4]{2,1,0:T(2,128)} %bitcast.44), calls=%async_computation.2 | async-start | bytes 16384 | tf_op jit(solution)/shard_map/all_to_all | solution.py:189
where the time goes:
time: 573 us; the launch traced here: 563 us
  waiting for transfers between devices  182 us (32%)
  local copies, waits for them, and re-layouts  161 us (28%)
  matrix products  131 us (23%)
  other arithmetic  59.5 us (10%)
  starting transfers between devices  16.1 us (3%)
  loops' own time  6.76 us (1%)
  blocking collectives  5.78 us (1%)
    all_to_all x1, waiting for transfers between devices, per_device(): lax.all_to_all(outgoing.reshape(vol_count, capacity, BOX ** 3), 'vol', sp...  176 us
    gather x45, local copies, waits for them, and re-layouts  97.7 us
    dot_general x152, matrix products, lower_product(): jnp.einsum(pattern, operand_a.astype(jnp.bfloat16), operand_b.astype(jnp....  95.7 us
    convert_element_type x8, other arithmetic, lower_product(): operand_a.astype(jnp.bfloat16)  33.2 us
    reshape x1, local copies, waits for them, and re-layouts, per_device(): box_rows.reshape(own_total, BOX ** 3)  22.8 us
    dot_general x26, matrix products, product(): jnp.einsum(pattern, operand_a, operand_b, precision=lax.Precision.HIGHEST)  21.8 us
    dynamic_update_slice x8, other arithmetic, candidates(): return lax.map(candidates_single, box_rows)  13.5 us
  transfers between devices with their start and end apart: 3, of which 2 were waited for; matrix products, arithmetic and copies ran while one was open for 25% of the time, Pallas kernels for 0%

commit v1 on v0

v1 whole, which is shorter than its diff:
```python
import math

import jax
import jax.numpy as jnp
from jax import lax
from jax.sharding import PartitionSpec as P

BOX = 64
TMPL = 32
SHIFT = 8
HALF = 33


epsilon = 1e-05


def shift_anchor():
    return (BOX - TMPL) // 2 - SHIFT // 2


def angle_of(turn_index):
    return turn_index.astype(jnp.float32) * (2.0 * math.pi / BOX)


def phases(count_out, count_in, offset):
    out_index = jnp.arange(count_out, dtype=jnp.int32) + offset
    in_index = jnp.arange(count_in, dtype=jnp.int32)
    turn_index = out_index[:, None] * in_index[None, :] % BOX
    phase_angle = angle_of(turn_index)
    return (jnp.cos(phase_angle), jnp.sin(phase_angle))


def bf(x):
    return x.astype(jnp.bfloat16)


def complex_table(cos_t, sin_t, sign_re_from_im, sign_im_from_re):
    c = bf(cos_t).T
    s = bf(sin_t).T
    re_row = jnp.stack([c, sign_im_from_re * s], axis=1)
    im_row = jnp.stack([sign_re_from_im * s, c], axis=1)
    return jnp.stack([re_row, im_row], axis=0)


def section(pattern, operand, table):
    return jnp.einsum(pattern, bf(operand), table, preferred_element_type=jnp.float32)


def forward_tail(stage_one):
    length_a = stage_one.shape[2]
    length_y = stage_one.shape[3]
    cos_full, sin_full = phases(BOX, length_y, 0)
    t_mid = complex_table(cos_full, sin_full, 1.0, -1.0)
    stage_two = section("ncayk,cydj->ndajk", stage_one, t_mid)
    cos_half, sin_half = phases(HALF, length_a, 0)
    t_first = complex_table(cos_half, sin_half, 1.0, -1.0)
    return section("ncajk,cadh->ndhjk", stage_two, t_first)


def template_spectra(cubes):
    volume = cubes.astype(jnp.float32)
    count = volume.shape[0]
    flat = volume.reshape(count, -1)
    centred = flat - jnp.mean(flat, axis=1, keepdims=True)
    unit = centred / jnp.sqrt(jnp.mean(centred * centred, axis=1, keepdims=True) + epsilon)
    unit = unit.reshape(count, TMPL, TMPL, TMPL)
    cos_full, sin_full = phases(BOX, TMPL, 0)
    t_last = jnp.stack([bf(cos_full).T, -bf(sin_full).T], axis=1)
    stage_one = section("nabx,xck->ncabk", unit, t_last)
    return bf(forward_tail(stage_one))


def window_table(corner_x, width):
    pos = jnp.arange(width, dtype=jnp.int32)[None, :] - corner_x[:, None]
    inside = (pos >= 0) & (pos < BOX)
    k = jnp.arange(BOX, dtype=jnp.int32)
    turn = k[None, None, :] * pos[:, :, None] % BOX
    phase_angle = angle_of(turn)
    mask = inside[:, :, None]
    cos_t = jnp.where(mask, bf(jnp.cos(phase_angle)), jnp.zeros((), jnp.bfloat16))
    sin_t = jnp.where(mask, -bf(jnp.sin(phase_angle)), jnp.zeros((), jnp.bfloat16))
    return jnp.stack([cos_t, sin_t], axis=2)


def band_table():
    lower_edge = jnp.arange(SHIFT, dtype=jnp.int32)[:, None] + shift_anchor()
    cell_index = jnp.arange(BOX, dtype=jnp.int32)[None, :]
    return ((cell_index >= lower_edge) & (cell_index < lower_edge + TMPL)).astype(jnp.float32)


def window_band(corner_x, width):
    lower_edge = jnp.arange(SHIFT, dtype=jnp.int32)[None, :, None] + shift_anchor() + corner_x[:, None, None]
    cell_index = jnp.arange(width, dtype=jnp.int32)[None, None, :]
    return ((cell_index >= lower_edge) & (cell_index < lower_edge + TMPL)).astype(jnp.float32)


def window_rms(rows, corner_x):
    width = rows.shape[-1]
    squares = rows.astype(jnp.float32) ** 2
    band_x = window_band(corner_x, width)
    band = band_table()
    hi = lax.Precision.HIGHEST
    sums_c = jnp.einsum("nabx,nux->nabu", squares, band_x, precision=hi)
    sums_b = jnp.einsum("nabu,tb->natu", sums_c, band, precision=hi)
    sums_a = jnp.einsum("natu,sa->nstu", sums_b, band, precision=hi)
    return jnp.sqrt(sums_a / float(TMPL**3) + epsilon)


def match(box_spectra, box_rms, spectra):
    values = lax.map(lambda one: match_one(box_spectra, box_rms, one[None]), spectra)
    return values[:, :, 0].T


def match_one(box_spectra, box_rms, spectra):
    real_t = spectra[:, 0].astype(jnp.float32)[None]
    imag_t = spectra[:, 1].astype(jnp.float32)[None]
    real_v = box_spectra[:, 0][:, None]
    imag_v = box_spectra[:, 1][:, None]
    real_p = real_t * real_v + imag_t * imag_v
    imag_p = real_t * imag_v - imag_t * real_v
    cross = jnp.stack([bf(real_p), bf(imag_p)], axis=2)
    cos_first, sin_first = phases(SHIFT, HALF, shift_anchor())
    freq_index = jnp.arange(HALF, dtype=jnp.int32)
    weight = jnp.where(freq_index % (BOX // 2) == 0, 1.0, 2.0) / float(BOX**3)
    cos_first = cos_first * weight[None, :]
    sin_first = sin_first * weight[None, :]
    t_first = complex_table(cos_first, sin_first, -1.0, 1.0)
    stage_g = section("nrchjk,chds->nrdsjk", cross, t_first)
    cos_rest, sin_rest = phases(SHIFT, BOX, shift_anchor())
    t_mid = complex_table(cos_rest, sin_rest, -1.0, 1.0)
    stage_h = section("nrcsjk,cjdt->nrdstk", stage_g, t_mid)
    t_last = jnp.stack([bf(cos_rest).T, -bf(sin_rest).T], axis=0)
    correlation = section("nrcstk,cku->nrstu", stage_h, t_last)
    scores = correlation / (box_rms[:, None] * math.sqrt(float(TMPL**3)))
    return jnp.max(scores, axis=(2, 3, 4))


def per_device(tomogram, templates, corner_z, corner_y, corner_x, loads):
    own_total = corner_z.shape[1]
    live_count = jnp.sum(loads[0, 0])
    width = tomogram.shape[2]

    def rows_of(cz, cy):
        return lax.dynamic_slice(tomogram, (cz, cy, 0), (BOX, BOX, width))

    rows = jax.vmap(rows_of)(corner_z[0], corner_y[0])
    t_last = window_table(corner_x[0], width)
    stage_one = jnp.einsum("nabx,nxck->ncabk", rows, t_last, preferred_element_type=jnp.float32)
    box_spectra = forward_tail(stage_one)
    box_rms = window_rms(rows, corner_x[0])

    all_templates = lax.all_gather(templates, "orient", axis=0, tiled=True)
    spectra = template_spectra(all_templates.reshape(-1, TMPL, TMPL, TMPL))
    values = match(box_spectra, box_rms, spectra)
    live = jnp.arange(own_total, dtype=jnp.int32) < live_count
    matched = jnp.where(live[:, None], values, 0.0)
    return (matched[None], jnp.max(matched, axis=1)[None])


def solution(mesh):
    return jax.shard_map(
        per_device,
        mesh=mesh,
        in_specs=(
            P("vol", "orient", None),
            P("orient", None, None),
            P("vol", "orient"),
            P("vol", "orient"),
            P("vol", "orient"),
            P("vol", "orient", None),
        ),
        out_specs=(P("vol", "orient", None), P("vol", "orient")),
        check_vma=False,
    )
```

time: 573 us -> 462 us (0.81); the launches traced: 563 us -> 459 us
  waiting for transfers between devices: 182 us -> 0 us
  matrix products: 131 us -> 202 us
  other arithmetic: 59.5 us -> 87.3 us
  starting transfers between devices: 16.1 us -> 0 us
  loops' own time: 6.76 us -> 0.33 us
    all_to_all x3 -> x0, waiting for transfers between devices: 182 us -> none  [the longest x1 176 us: per_device(): lax.all_to_all(outgoing.reshape(vol_count, capacity, BOX ** 3), 'vol', sp...]
    dot_general x180 -> x21, matrix products: 131 us -> 202 us  [the longest x17 123 us: section(): jnp.einsum(pattern, bf(operand), table, preferred_element_type=jnp.float32)]
    another operation x3 -> x16, other arithmetic: 0.98 us -> 71.6 us  [the longest x4 71.5 us: match_one(): cross = jnp.stack([bf(real_p), bf(imag_p)], axis=2)]
    convert_element_type x6 -> x4, local copies, waits for them, and re-layouts: 0.88 us -> 63.1 us  [the longest x3 61 us: bf(): return x.astype(jnp.bfloat16)]
    reshape x3 -> x0, local copies, waits for them, and re-layouts: 39.6 us -> none  [the longest x1 22.8 us: per_device(): box_rows.reshape(own_total, BOX ** 3)]
    convert_element_type x11 -> x17, other arithmetic: 34.6 us -> 1.94 us  [bf(): return x.astype(jnp.bfloat16)]
    all_to_all x3 -> x0, starting transfers between devices: 16.1 us -> none  [the longest x1 7.31 us: per_device(): lax.all_to_all(live_flags, 'vol', split_axis=0, concat_axis=0, tiled=True)]
    dynamic_update_slice x8 -> x0, other arithmetic: 13.5 us -> none  [candidates(): return lax.map(candidates_single, box_rows)]
  transfers between devices with their start and end apart: 3 -> 0, of which waited for: 2 -> 0; matrix products, arithmetic and copies ran while one was open for 25% -> 0% of each run, Pallas kernels for 0% -> 0%
where the time goes in v1:
time: 462 us; the launch traced here: 459 us
  matrix products  202 us (44%)
  local copies, waits for them, and re-layouts  161 us (35%)
  other arithmetic  87.3 us (19%)
  blocking collectives  7.43 us (2%)
    dot_general x17, matrix products, section(): jnp.einsum(pattern, bf(operand), table, preferred_element_type=jnp.float32)  123 us
    gather x45, local copies, waits for them, and re-layouts  92.2 us
    another operation x4, other arithmetic, match_one(): cross = jnp.stack([bf(real_p), bf(imag_p)], axis=2)  71.5 us
    convert_element_type x3, local copies, waits for them, and re-layouts, bf(): return x.astype(jnp.bfloat16)  61 us
    dot_general x1, matrix products, window_rms(): sums_c = jnp.einsum('nabx,nux->nabu', squares, band_x, precision=hi)  43.2 us
    dot_general x1, matrix products, per_device(): jnp.einsum('nabx,nxck->ncabk', rows, t_last, preferred_element_type=jnp.f...  29 us

profile of v1, /device:TPU:0, one launch (start us, length us, event | category | flops | bytes accessed | tf_op | source)
XLA Modules:
  0.0 459.2 jit_solution(9681375477031714655)
XLA Ops:
  0.6 1.4 reduce_sum.27
  2.0 1.2 iota_compare_fusion.5
  7.2 7.4 %all_gather.3 = bf16[4,32,1024]{2,1,0:T(8,128)(2,1)S(1)} all-gather(bf16[1,32,1024]{2,1,0:T(8,128)(2,1)} %param.9), channel_id=1, replica_groups=mesh['vol'=8,'orient'=4] {'orient'}, dimensions={0}, use_global_device_ids=true | all-gather | bytes 327680 | tf_op jit(solution)/shard_map/all_gather | solution.py:152
  15.1 4.2 fusion.99
  19.3 2.0 reshape.1145
  21.3 2.3 convert_bitcast_fusion.1
  23.7 6.8 %copy.50 = bf16[4,2,32,32,64]{3,2,1,4,0:T(8,128)(2,1)} copy(bf16[4,2,32,32,64]{4,3,2,0,1:T(8,128)(2,1)S(1)} %convert_bitcast_fusion.1) | data formatting | bytes 2097152 | tf_op jit(solution)/shard_map/convert_element_type | solution.py:34
  30.5 5.4 %fusion.71 = bf16[4,2,32,64,64]{3,2,4,0,1:T(8,128)(2,1)} fusion(bf16[4,2,32,32,64]{3,2,1,4,0:T(8,128)(2,1)} %copy.50, bf16[1,32,2,64]{3,1,2,0:T(8,128)(2,1)S(1)} %get-tuple-element.159, bf16[1,32,2,64]{3,1,2,0:T(8,128)(2,1)S(1)} %get-tuple-element.158), kind=kOutput, calls=%fused_computation.101 | convolution fusion | flops 135274496 | bytes 3162112 | tf_op jit(solution)/shard_map/ncayk,cydj->ndajk/dot_general | solution.py:46
  35.9 10.9 %copy.51 = bf16[4,2,32,64,64]{4,2,1,3,0:T(8,128)(2,1)} copy(bf16[4,2,32,64,64]{3,2,4,0,1:T(8,128)(2,1)} %fusion.71) | data formatting | bytes 4194304 | tf_op jit(solution)/shard_map/convert_element_type | solution.py:34
  46.8 6.0 %fusion.70 = bf16[4,2,33,64,64]{4,2,3,0,1:T(8,128)(2,1)} fusion(bf16[4,2,32,64,64]{4,2,1,3,0:T(8,128)(2,1)} %copy.51, bf16[1,32,2,33]{3,1,0,2:T(8,128)(2,1)S(1)} %get-tuple-element.157, bf16[1,32,2,33]{3,1,0,2:T(8,128)(2,1)S(1)} %get-tuple-element.156), kind=kOutput, calls=%fused_computation.100 | convolution fusion | flops 139510272 | bytes 4268288 | tf_op jit(solution)/shard_map/ncajk,cadh->ndhjk/dot_general | solution.py:46
  52.9 92.2 %while.15 = (s32[]{:T(128)}, bf16[80,128,256]{2,1,0:T(8,128)(2,1)}, s32[15,3]{0,1:T(4,128)S(1)}, bf16[15,64,64,256]{3,2,1,0:T(8,128)(2,1)}, s32[]{:T(128)}) while((s32[]{:T(128)}, bf16[80,128,256]{2,1,0:T(8,128)(2,1)}, s32[15,3]{0,1:T(4,128)S(1)}, bf16[15,64,64,256]{3,2,1,0:T(8,128)(2,1)}, s32[]{:T(128)}) %tuple.81), condition=%wide.while_cond, body=%wide.while_body.sunk | while | flops 2 | bytes 4195445 | solution.py:144
  53.5 5.5 %bitcast_dynamic-update-slice_fusion.5 = bf16[15,64,64,256]{3,2,1,0:T(8,128)(2,1)} fusion(bf16[15,64,64,256]{3,2,1,0:T(8,128)(2,1)} %get-tuple-element.266, s32[]{:T(128)S(6)} %copy.116, bf16[80,128,256]{2,1,0:T(8,128)(2,1)} %get-tuple-element.269, s32[]{:T(128)} %bitcast.270, s32[]{:T(128)} %bitcast.271), kind=kLoop, calls=%fused_computation.82.clone.1 | loop fusion | bytes 4195332 | tf_op jit(solution)/shard_map/vmap()/gather
  59.7 5.5 %bitcast_dynamic-update-slice_fusion.5 = bf16[15,64,64,256]{3,2,1,0:T(8,128)(2,1)} fusion(bf16[15,64,64,256]{3,2,1,0:T(8,128)(2,1)} %get-tuple-element.266, s32[]{:T(128)S(6)} %copy.116, bf16[80,128,256]{2,1,0:T(8,128)(2,1)} %get-tuple-element.269, s32[]{:T(128)} %bitcast.270, s32[]{:T(128)} %bitcast.271), kind=kLoop, calls=%fused_computation.82.clone.1 | loop fusion | bytes 4195332 | tf_op jit(solution)/shard_map/vmap()/gather
  65.9 5.5 %bitcast_dynamic-update-slice_fusion.5 = bf16[15,64,64,256]{3,2,1,0:T(8,128)(2,1)} fusion(bf16[15,64,64,256]{3,2,1,0:T(8,128)(2,1)} %get-tuple-element.266, s32[]{:T(128)S(6)} %copy.116, bf16[80,128,256]{2,1,0:T(8,128)(2,1)} %get-tuple-element.269, s32[]{:T(128)} %bitcast.270, s32[]{:T(128)} %bitcast.271), kind=kLoop, calls=%fused_computation.82.clone.1 | loop fusion | bytes 4195332 | tf_op jit(solution)/shard_map/vmap()/gather
  72.0 5.6 %bitcast_dynamic-update-slice_fusion.5 = bf16[15,64,64,256]{3,2,1,0:T(8,128)(2,1)} fusion(bf16[15,64,64,256]{3,2,1,0:T(8,128)(2,1)} %get-tuple-element.266, s32[]{:T(128)S(6)} %copy.116, bf16[80,128,256]{2,1,0:T(8,128)(2,1)} %get-tuple-element.269, s32[]{:T(128)} %bitcast.270, s32[]{:T(128)} %bitcast.271), kind=kLoop, calls=%fused_computation.82.clone.1 | loop fusion | bytes 4195332 | tf_op jit(solution)/shard_map/vmap()/gather
  78.2 5.4 %bitcast_dynamic-update-slice_fusion.5 = bf16[15,64,64,256]{3,2,1,0:T(8,128)(2,1)} fusion(bf16[15,64,64,256]{3,2,1,0:T(8,128)(2,1)} %get-tuple-element.266, s32[]{:T(128)S(6)} %copy.116, bf16[80,128,256]{2,1,0:T(8,128)(2,1)} %get-tuple-element.269, s32[]{:T(128)} %bitcast.270, s32[]{:T(128)} %bitcast.271), kind=kLoop, calls=%fused_computation.82.clone.1 | loop fusion | bytes 4195332 | tf_op jit(solution)/shard_map/vmap()/gather
  84.3 5.4 %bitcast_dynamic-update-slice_fusion.5 = bf16[15,64,64,256]{3,2,1,0:T(8,128)(2,1)} fusion(bf16[15,64,64,256]{3,2,1,0:T(8,128)(2,1)} %get-tuple-element.266, s32[]{:T(128)S(6)} %copy.116, bf16[80,128,256]{2,1,0:T(8,128)(2,1)} %get-tuple-element.269, s32[]{:T(128)} %bitcast.270, s32[]{:T(128)} %bitcast.271), kind=kLoop, calls=%fused_computation.82.clone.1 | loop fusion | bytes 4195332 | tf_op jit(solution)/shard_map/vmap()/gather
  90.4 5.5 %bitcast_dynamic-update-slice_fusion.5 = bf16[15,64,64,256]{3,2,1,0:T(8,128)(2,1)} fusion(bf16[15,64,64,256]{3,2,1,0:T(8,128)(2,1)} %get-tuple-element.266, s32[]{:T(128)S(6)} %copy.116, bf16[80,128,256]{2,1,0:T(8,128)(2,1)} %get-tuple-element.269, s32[]{:T(128)} %bitcast.270, s32[]{:T(128)} %bitcast.271), kind=kLoop, calls=%fused_computation.82.clone.1 | loop fusion | bytes 4195332 | tf_op jit(solution)/shard_map/vmap()/gather
  96.6 5.5 %bitcast_dynamic-update-slice_fusion.5 = bf16[15,64,64,256]{3,2,1,0:T(8,128)(2,1)} fusion(bf16[15,64,64,256]{3,2,1,0:T(8,128)(2,1)} %get-tuple-element.266, s32[]{:T(128)S(6)} %copy.116, bf16[80,128,256]{2,1,0:T(8,128)(2,1)} %get-tuple-element.269, s32[]{:T(128)} %bitcast.270, s32[]{:T(128)} %bitcast.271), kind=kLoop, calls=%fused_computation.82.clone.1 | loop fusion | bytes 4195332 | tf_op jit(solution)/shard_map/vmap()/gather
  102.7 5.5 %bitcast_dynamic-update-slice_fusion.5 = bf16[15,64,64,256]{3,2,1,0:T(8,128)(2,1)} fusion(bf16[15,64,64,256]{3,2,1,0:T(8,128)(2,1)} %get-tuple-element.266, s32[]{:T(128)S(6)} %copy.116, bf16[80,128,256]{2,1,0:T(8,128)(2,1)} %get-tuple-element.269, s32[]{:T(128)} %bitcast.270, s32[]{:T(128)} %bitcast.271), kind=kLoop, calls=%fused_computation.82.clone.1 | loop fusion | bytes 4195332 | tf_op jit(solution)/shard_map/vmap()/gather
  108.9 5.5 %bitcast_dynamic-update-slice_fusion.5 = bf16[15,64,64,256]{3,2,1,0:T(8,128)(2,1)} fusion(bf16[15,64,64,256]{3,2,1,0:T(8,128)(2,1)} %get-tuple-element.266, s32[]{:T(128)S(6)} %copy.116, bf16[80,128,256]{2,1,0:T(8,128)(2,1)} %get-tuple-element.269, s32[]{:T(128)} %bitcast.270, s32[]{:T(128)} %bitcast.271), kind=kLoop, calls=%fused_computation.82.clone.1 | loop fusion | bytes 4195332 | tf_op jit(solution)/shard_map/vmap()/gather
  115.0 5.5 %bitcast_dynamic-update-slice_fusion.5 = bf16[15,64,64,256]{3,2,1,0:T(8,128)(2,1)} fusion(bf16[15,64,64,256]{3,2,1,0:T(8,128)(2,1)} %get-tuple-element.266, s32[]{:T(128)S(6)} %copy.116, bf16[80,128,256]{2,1,0:T(8,128)(2,1)} %get-tuple-element.269, s32[]{:T(128)} %bitcast.270, s32[]{:T(128)} %bitcast.271), kind=kLoop, calls=%fused_computation.82.clone.1 | loop fusion | bytes 4195332 | tf_op jit(solution)/shard_map/vmap()/gather
  121.2 5.6 %bitcast_dynamic-update-slice_fusion.5 = bf16[15,64,64,256]{3,2,1,0:T(8,128)(2,1)} fusion(bf16[15,64,64,256]{3,2,1,0:T(8,128)(2,1)} %get-tuple-element.266, s32[]{:T(128)S(6)} %copy.116, bf16[80,128,256]{2,1,0:T(8,128)(2,1)} %get-tuple-element.269, s32[]{:T(128)} %bitcast.270, s32[]{:T(128)} %bitcast.271), kind=kLoop, calls=%fused_computation.82.clone.1 | loop fusion | bytes 4195332 | tf_op jit(solution)/shard_map/vmap()/gather
  127.4 5.4 %bitcast_dynamic-update-slice_fusion.5 = bf16[15,64,64,256]{3,2,1,0:T(8,128)(2,1)} fusion(bf16[15,64,64,256]{3,2,1,0:T(8,128)(2,1)} %get-tuple-element.266, s32[]{:T(128)S(6)} %copy.116, bf16[80,128,256]{2,1,0:T(8,128)(2,1)} %get-tuple-element.269, s32[]{:T(128)} %bitcast.270, s32[]{:T(128)} %bitcast.271), kind=kLoop, calls=%fused_computation.82.clone.1 | loop fusion | bytes 4195332 | tf_op jit(solution)/shard_map/vmap()/gather
  133.5 5.4 %bitcast_dynamic-update-slice_fusion.5 = bf16[15,64,64,256]{3,2,1,0:T(8,128)(2,1)} fusion(bf16[15,64,64,256]{3,2,1,0:T(8,128)(2,1)} %get-tuple-element.266, s32[]{:T(128)S(6)} %copy.116, bf16[80,128,256]{2,1,0:T(8,128)(2,1)} %get-tuple-element.269, s32[]{:T(128)} %bitcast.270, s32[]{:T(128)} %bitcast.271), kind=kLoop, calls=%fused_computation.82.clone.1 | loop fusion | bytes 4195332 | tf_op jit(solution)/shard_map/vmap()/gather
  139.6 5.5 %bitcast_dynamic-update-slice_fusion.5 = bf16[15,64,64,256]{3,2,1,0:T(8,128)(2,1)} fusion(bf16[15,64,64,256]{3,2,1,0:T(8,128)(2,1)} %get-tuple-element.266, s32[]{:T(128)S(6)} %copy.116, bf16[80,128,256]{2,1,0:T(8,128)(2,1)} %get-tuple-element.269, s32[]{:T(128)} %bitcast.270, s32[]{:T(128)} %bitcast.271), kind=kLoop, calls=%fused_computation.82.clone.1 | loop fusion | bytes 4195332 | tf_op jit(solution)/shard_map/vmap()/gather
  145.1 43.2 %fusion.52 = f32[15,64,64,8]{2,3,1,0:T(8,128)S(1)} fusion(bf16[15,64,64,256]{3,2,1,0:T(8,128)(2,1)} %get-tuple-element.97, s32[15,8]{1,0:T(8,128)S(1)} %get-tuple-element.163, s32[15,8]{1,0:T(8,128)S(1)} %get-tuple-element.162), kind=kOutput, calls=%fused_computation.85 | convolution fusion | flops 1541498880 | bytes 33424320 | tf_op jit(solution)/shard_map/nabx,nux->nabu/dot_general | solution.py:103
  188.2 4.7 %fusion.82 = f32[15,64,8,8]{1,2,3,0:T(8,128)S(1)} fusion(f32[15,64,64,8]{2,3,1,0:T(8,128)S(1)} %fusion.52, s32[8]{0:T(128)S(1)} %get-tuple-element.172, s32[8]{0:T(128)S(1)} %get-tuple-element.173), kind=kOutput, calls=%fused_computation.113 | convolution fusion | flops 47187456 | bytes 2211904 | tf_op jit(solution)/shard_map/nabu,tb->natu/dot_general | solution.py:104
  192.9 29.0 %convert_bitcast_fusion = bf16[15,2,64,64,64]{3,4,2,1,0:T(8,128)(2,1)} fusion(bf16[15,64,64,256]{3,2,1,0:T(8,128)(2,1)} %get-tuple-element.97, bf16[15,256,1,64]{1,3,2,0:T(8,128)(2,1)S(1)} %get-tuple-element.151, bf16[15,256,1,64]{1,3,2,0:T(8,128)(2,1)S(1)} %get-tuple-element.150), kind=kOutput, calls=%fused_computation.96 | convolution fusion | flops 4036362240 | bytes 48168960 | tf_op jit(solution)/shard_map/nabx,nxck->ncabk/dot_general | solution.py:148
  221.9 2.0 fusion.87
  223.9 54.2 %fusion.55 = bf16[15,2,64,64,64]{2,3,4,0,1:T(8,128)(2,1)} fusion(bf16[15,2,64,64,64]{3,4,2,1,0:T(8,128)(2,1)} %convert_bitcast_fusion, bf16[1,64,2,64]{1,3,0,2:T(8,128)(2,1)S(1)} %get-tuple-element.153, bf16[1,64,2,64]{1,3,0,2:T(8,128)(2,1)S(1)} %get-tuple-element.152), kind=kOutput, calls=%fused_computation.88 | convolution fusion | flops 2021195776 | bytes 31490048 | tf_op jit(solution)/shard_map/ncayk,cydj->ndajk/dot_general | solution.py:46
  278.0 43.3 %copy.55 = bf16[15,2,64,64,64]{4,2,1,3,0:T(8,128)(2,1)} copy(bf16[15,2,64,64,64]{2,3,4,0,1:T(8,128)(2,1)} %fusion.55) | data formatting | bytes 31457280 | tf_op jit(solution)/shard_map/convert_element_type | solution.py:34
  321.4 24.2 %fusion.67 = f32[15,2,33,64,64]{4,2,3,0,1:T(8,128)} fusion(bf16[15,2,64,64,64]{4,2,1,3,0:T(8,128)(2,1)} %copy.55, bf16[1,64,2,33]{1,3,0,2:T(8,128)(2,1)S(1)} %get-tuple-element.155, bf16[1,64,2,33]{1,3,0,2:T(8,128)(2,1)S(1)} %get-tuple-element.154), kind=kOutput, calls=%fused_computation.97 | convolution fusion | flops 1038124032 | bytes 31965696 | tf_op jit(solution)/shard_map/ncajk,cadh->ndhjk/dot_general | solution.py:46
  345.5 112.5 %while.14 = (s32[]{:T(128)}, f32[4,15,1]{1,2,0:T(1,128)S(1)}, bf16[4,2,33,64,64]{4,2,3,0,1:T(8,128)(2,1)}, f32[15,2,33,64,64]{4,2,3,0,1:T(8,128)}, f32[15,8,8,8]{0,3,2,1:T(8,128)S(1)}, /*index=5*/s32[]{:T(128)}) while((s32[]{:T(128)}, f32[4,15,1]{1,2,0:T(1,128)S(1)}, bf16[4,2,33,64,64]{4,2,3,0,1:T(8,128)(2,1)}, ...), condition=%wide.region_5.6_spmd, body=%wide.region_3.5_spmd.sunk | while | flops 197085936 | bytes 40707036 | solution.py:110
  346.3 1.4 dynamic-slice_bitcast_fusion.2
  347.9 17.9 %fusion.171 = (bf16[15,1,1,33,64,64]{5,3,2,4,0,1:T(8,128)(2,1)S(1)}, bf16[15,1,1,33,64,64]{5,3,2,4,0,1:T(8,128)(2,1)}) fusion(f32[15,2,33,64,64]{4,2,3,0,1:T(8,128)} %get-tuple-element.288, f32[33,64,64]{2,0,1:T(8,128)S(1)} %get-tuple-element.240, f32[33,64,64]{2,0,1:T(8,128)S(1)} %get-tuple-element.241), kind=kLoop, calls=%fused_computation.6.clone.1 | loop fusion | flops 16220160 | bytes 25411584 | tf_op jit(solution)/shard_map/while/body/eval_jaxpr/stack | solution.py:121
  365.8 6.4 %fusion.173 = bf16[15,2,8,64,64]{4,2,3,0,1:T(8,128)(2,1)S(1)} fusion(bf16[15,1,1,33,64,64]{5,3,2,4,0,1:T(8,128)(2,1)} %get-tuple-element.242, bf16[15,1,1,33,64,64]{5,3,2,4,0,1:T(8,128)(2,1)S(1)} %get-tuple-element.243, bf16[1,33,2,8]{1,3,0,2:T(8,128)(2,1)S(1)} %get-tuple-element.246, bf16[1,33,2,8]{1,3,0,2:T(8,128)(2,1)S(1)} %get-tuple-element.247), kind=kOutput, calls=%fused_computation.9.clone.1 | convolution fusion | flops 146968704 | bytes 10078272 | tf_op jit(solution)/shard_map/while/body/eval_jaxpr/nrchjk,chds->nrdsjk/dot_general | solution.py:46
  372.9 0.8 fusion.176
  374.5 1.4 dynamic-slice_bitcast_fusion.2
  376.1 17.9 %fusion.171 = (bf16[15,1,1,33,64,64]{5,3,2,4,0,1:T(8,128)(2,1)S(1)}, bf16[15,1,1,33,64,64]{5,3,2,4,0,1:T(8,128)(2,1)}) fusion(f32[15,2,33,64,64]{4,2,3,0,1:T(8,128)} %get-tuple-element.288, f32[33,64,64]{2,0,1:T(8,128)S(1)} %get-tuple-element.240, f32[33,64,64]{2,0,1:T(8,128)S(1)} %get-tuple-element.241), kind=kLoop, calls=%fused_computation.6.clone.1 | loop fusion | flops 16220160 | bytes 25411584 | tf_op jit(solution)/shard_map/while/body/eval_jaxpr/stack | solution.py:121
  393.9 6.4 %fusion.173 = bf16[15,2,8,64,64]{4,2,3,0,1:T(8,128)(2,1)S(1)} fusion(bf16[15,1,1,33,64,64]{5,3,2,4,0,1:T(8,128)(2,1)} %get-tuple-element.242, bf16[15,1,1,33,64,64]{5,3,2,4,0,1:T(8,128)(2,1)S(1)} %get-tuple-element.243, bf16[1,33,2,8]{1,3,0,2:T(8,128)(2,1)S(1)} %get-tuple-element.246, bf16[1,33,2,8]{1,3,0,2:T(8,128)(2,1)S(1)} %get-tuple-element.247), kind=kOutput, calls=%fused_computation.9.clone.1 | convolution fusion | flops 146968704 | bytes 10078272 | tf_op jit(solution)/shard_map/while/body/eval_jaxpr/nrchjk,chds->nrdsjk/dot_general | solution.py:46
  402.6 1.4 dynamic-slice_bitcast_fusion.2
  404.2 17.9 %fusion.171 = (bf16[15,1,1,33,64,64]{5,3,2,4,0,1:T(8,128)(2,1)S(1)}, bf16[15,1,1,33,64,64]{5,3,2,4,0,1:T(8,128)(2,1)}) fusion(f32[15,2,33,64,64]{4,2,3,0,1:T(8,128)} %get-tuple-element.288, f32[33,64,64]{2,0,1:T(8,128)S(1)} %get-tuple-element.240, f32[33,64,64]{2,0,1:T(8,128)S(1)} %get-tuple-element.241), kind=kLoop, calls=%fused_computation.6.clone.1 | loop fusion | flops 16220160 | bytes 25411584 | tf_op jit(solution)/shard_map/while/body/eval_jaxpr/stack | solution.py:121
  422.1 6.4 %fusion.173 = bf16[15,2,8,64,64]{4,2,3,0,1:T(8,128)(2,1)S(1)} fusion(bf16[15,1,1,33,64,64]{5,3,2,4,0,1:T(8,128)(2,1)} %get-tuple-element.242, bf16[15,1,1,33,64,64]{5,3,2,4,0,1:T(8,128)(2,1)S(1)} %get-tuple-element.243, bf16[1,33,2,8]{1,3,0,2:T(8,128)(2,1)S(1)} %get-tuple-element.246, bf16[1,33,2,8]{1,3,0,2:T(8,128)(2,1)S(1)} %get-tuple-element.247), kind=kOutput, calls=%fused_computation.9.clone.1 | convolution fusion | flops 146968704 | bytes 10078272 | tf_op jit(solution)/shard_map/while/body/eval_jaxpr/nrchjk,chds->nrdsjk/dot_general | solution.py:46
  430.7 1.4 dynamic-slice_bitcast_fusion.2
  432.3 17.9 %fusion.171 = (bf16[15,1,1,33,64,64]{5,3,2,4,0,1:T(8,128)(2,1)S(1)}, bf16[15,1,1,33,64,64]{5,3,2,4,0,1:T(8,128)(2,1)}) fusion(f32[15,2,33,64,64]{4,2,3,0,1:T(8,128)} %get-tuple-element.288, f32[33,64,64]{2,0,1:T(8,128)S(1)} %get-tuple-element.240, f32[33,64,64]{2,0,1:T(8,128)S(1)} %get-tuple-element.241), kind=kLoop, calls=%fused_computation.6.clone.1 | loop fusion | flops 16220160 | bytes 25411584 | tf_op jit(solution)/shard_map/while/body/eval_jaxpr/stack | solution.py:121
  450.2 6.4 %fusion.173 = bf16[15,2,8,64,64]{4,2,3,0,1:T(8,128)(2,1)S(1)} fusion(bf16[15,1,1,33,64,64]{5,3,2,4,0,1:T(8,128)(2,1)} %get-tuple-element.242, bf16[15,1,1,33,64,64]{5,3,2,4,0,1:T(8,128)(2,1)S(1)} %get-tuple-element.243, bf16[1,33,2,8]{1,3,0,2:T(8,128)(2,1)S(1)} %get-tuple-element.246, bf16[1,33,2,8]{1,3,0,2:T(8,128)(2,1)S(1)} %get-tuple-element.247), kind=kOutput, calls=%fused_computation.9.clone.1 | convolution fusion | flops 146968704 | bytes 10078272 | tf_op jit(solution)/shard_map/while/body/eval_jaxpr/nrchjk,chds->nrdsjk/dot_general | solution.py:46
  458.1 1.1 select_reduce_fusion
  (115 shorter events, 22.9 us)
Async XLA Ops:
  345.5 112.5 %copy-start = (pred[15]{0:T(512)(128)(4,1)S(1)}, pred[15]{0:T(512)(128)(4,1)}, u32[]{:S(2)}) copy-start(pred[15]{0:T(512)(128)(4,1)} %iota_compare_fusion.5) | copy-start | bytes 49

commit v2 on v1

--- a/solution.py
+++ b/solution.py
@@ -4,6 +4,8 @@
 import jax.numpy as jnp
 from jax import lax
 from jax.sharding import PartitionSpec as P
+from jax.experimental import pallas as pl
+from jax.experimental.pallas import tpu as pltpu
 
 BOX = 64
 TMPL = 32
@@ -135,23 +137,164 @@
     return jnp.max(scores, axis=(2, 3, 4))
 
 
+def front_kernel(cz_ref, slab_ref, t1_ref, l2_ref, ymask_ref, bxt_ref, q2_ref, rsum_ref, w_scr, y_scr):
+    depth, rows_y, width = slab_ref.shape
+    chunk = 8
+    t1 = t1_ref[...]
+    l2 = l2_ref[...]
+
+    def transform_chunk(ci, carry):
+        z0 = pl.multiple_of(ci * chunk, chunk)
+        rows = slab_ref[pl.ds(z0, chunk)].reshape(chunk * rows_y, width)
+        p1 = jnp.dot(rows, t1, preferred_element_type=jnp.float32)
+        p1 = p1.astype(jnp.bfloat16).astype(jnp.float32).reshape(chunk, rows_y, 2 * BOX)
+        p1t = jnp.swapaxes(p1, 1, 2).reshape(chunk * 2 * BOX, rows_y).astype(jnp.bfloat16)
+        m2 = jnp.dot(p1t, l2, preferred_element_type=jnp.float32).reshape(chunk, 2, BOX, 2 * BOX)
+        part_a = m2[:, 0]
+        part_b = m2[:, 1]
+        lane = lax.broadcasted_iota(jnp.int32, part_a.shape, 2)
+        sign = jnp.where(lane < BOX, 1.0, -1.0).astype(jnp.float32)
+        out = pltpu.roll(part_b, BOX, 2) + sign * part_a
+        q2_ref[pl.ds(z0, chunk)] = out.astype(jnp.bfloat16)
+        return carry
+
+    lax.fori_loop(0, depth // chunk, transform_chunk, 0)
+
+    lo_z = shift_anchor()
+
+    def plane_sq(z):
+        v = slab_ref[z].astype(jnp.float32)
+        return v * v
+
+    def first_window(z, acc):
+        return acc + plane_sq(lo_z + z)
+
+    acc = lax.fori_loop(0, TMPL, first_window, jnp.zeros((rows_y, width), jnp.float32))
+    w_scr[0] = acc
+    for s_i in range(1, SHIFT):
+        acc = acc + plane_sq(lo_z + TMPL + s_i - 1) - plane_sq(lo_z + s_i - 1)
+        w_scr[s_i] = acc
+
+    ymask = ymask_ref[...]
+
+    def y_sums(s_i, carry):
+        plane = w_scr[s_i]
+        for t_i in range(SHIFT):
+            y_scr[pl.ds(s_i * SHIFT + t_i, 1), :] = jnp.sum(plane * ymask[:, t_i:t_i + 1], axis=0, keepdims=True)
+        return carry
+
+    lax.fori_loop(0, SHIFT, y_sums, 0)
+    ysum = y_scr[...]
+    hi = ysum.astype(jnp.bfloat16)
+    rest = ysum - hi.astype(jnp.float32)
+    mid = rest.astype(jnp.bfloat16)
+    lo = (rest - mid.astype(jnp.float32)).astype(jnp.bfloat16)
+    bxt = bxt_ref[...]
+    total = jnp.dot(hi, bxt, preferred_element_type=jnp.float32)
+    total = total + jnp.dot(mid, bxt, preferred_element_type=jnp.float32)
+    total = total + jnp.dot(lo, bxt, preferred_element_type=jnp.float32)
+    rsum_ref[...] = total
+
+
+def front(tomogram, corner_z, corner_y, corner_x):
+    count = corner_z.shape[0]
+    rows_y = tomogram.shape[1]
+    width = tomogram.shape[2]
+    t1 = window_table(corner_x, width).reshape(count, width, 2 * BOX)
+    pos_y = jnp.arange(rows_y, dtype=jnp.int32)[None, :] - corner_y[:, None]
+    inside_y = (pos_y >= 0) & (pos_y < BOX)
+    j = jnp.arange(BOX, dtype=jnp.int32)
+    turn_y = pos_y[:, :, None] * j[None, None, :] % BOX
+    angle_y = angle_of(turn_y)
+    zero = jnp.zeros((), jnp.bfloat16)
+    cos_y = jnp.where(inside_y[:, :, None], bf(jnp.cos(angle_y)), zero)
+    sin_y = jnp.where(inside_y[:, :, None], bf(jnp.sin(angle_y)), zero)
+    l2 = jnp.concatenate([cos_y, sin_y], axis=2)
+    lower_y = jnp.arange(SHIFT, dtype=jnp.int32)[None, None, :] + shift_anchor() + corner_y[:, None, None]
+    cell_y = jnp.arange(rows_y, dtype=jnp.int32)[None, :, None]
+    ymask = ((cell_y >= lower_y) & (cell_y < lower_y + TMPL)).astype(jnp.float32)
+    bxt = jnp.swapaxes(window_band(corner_x, width), 1, 2).astype(jnp.bfloat16)
+
+    grid_spec = pltpu.PrefetchScalarGridSpec(
+        num_scalar_prefetch=1,
+        grid=(count,),
+        in_specs=[
+            pl.BlockSpec((pl.Element(BOX), pl.Element(rows_y), pl.Element(width)), lambda n, cz: (cz[n], 0, 0)),
+            pl.BlockSpec((None, width, 2 * BOX), lambda n, cz: (n, 0, 0)),
+            pl.BlockSpec((None, rows_y, 2 * BOX), lambda n, cz: (n, 0, 0)),
+            pl.BlockSpec((None, rows_y, SHIFT), lambda n, cz: (n, 0, 0)),
+            pl.BlockSpec((None, width, SHIFT), lambda n, cz: (n, 0, 0)),
+        ],
+        out_specs=[
+            pl.BlockSpec((None, BOX, BOX, 2 * BOX), lambda n, cz: (n, 0, 0, 0)),
+            pl.BlockSpec((None, SHIFT * SHIFT, SHIFT), lambda n, cz: (n, 0, 0)),
+        ],
+        scratch_shapes=[
+            pltpu.VMEM((SHIFT, rows_y, width), jnp.float32),
+            pltpu.VMEM((SHIFT * SHIFT, width), jnp.float32),
+        ],
+    )
+    q2, rsum = pl.pallas_call(
+        front_kernel,
+        grid_spec=grid_spec,
+        out_shape=[
+            jax.ShapeDtypeStruct((count, BOX, BOX, 2 * BOX), jnp.bfloat16),
+            jax.ShapeDtypeStruct((count, SHIFT * SHIFT, SHIFT), jnp.float32),
+        ],
+        compiler_params=pltpu.CompilerParams(vmem_limit_bytes=48 * 1024 * 1024),
+    )(corner_z, tomogram, t1, l2, ymask, bxt)
+    box_rms = jnp.sqrt(rsum.reshape(count, SHIFT, SHIFT, SHIFT) / float(TMPL**3) + epsilon)
+    return q2, box_rms
+
+
+def box_spectra_of(q2):
+    cos_half, sin_half = phases(HALF, BOX, 0)
+    l3 = jnp.concatenate([bf(cos_half), bf(sin_half)], axis=0)
+    m3 = jnp.einsum("nzkq,wz->nwkq", q2, l3, preferred_element_type=jnp.float32)
+    top = m3[:, :HALF]
+    bottom = m3[:, HALF:]
+    real = top[..., :BOX] + bottom[..., BOX:]
+    imag = top[..., BOX:] - bottom[..., :BOX]
+    return real, imag
+
+
+def match_kj(real_v, imag_v, box_rms, spectra):
+    spectra_kj = jnp.swapaxes(spectra, 3, 4)
+
+    def one(spectrum):
+        real_t = spectrum[0].astype(jnp.float32)[None, None]
+        imag_t = spectrum[1].astype(jnp.float32)[None, None]
+        rv = real_v[:, None]
+        iv = imag_v[:, None]
+        real_p = real_t * rv + imag_t * iv
+        imag_p = real_t * iv - imag_t * rv
+        cross = jnp.stack([bf(real_p), bf(imag_p)], axis=2)
+        cos_first, sin_first = phases(SHIFT, HALF, shift_anchor())
+        freq_index = jnp.arange(HALF, dtype=jnp.int32)
+        weight = jnp.where(freq_index % (BOX // 2) == 0, 1.0, 2.0) / float(BOX**3)
+        t_first = complex_table(cos_first * weight[None, :], sin_first * weight[None, :], -1.0, 1.0)
+        stage_g = section("nrchkj,chds->nrdskj", cross, t_first)
+        cos_rest, sin_rest = phases(SHIFT, BOX, shift_anchor())
+        t_mid = complex_table(cos_rest, sin_rest, -1.0, 1.0)
+        stage_h = section("nrcskj,cjdt->nrdskt", stage_g, t_mid)
+        t_last = jnp.stack([bf(cos_rest).T, -bf(sin_rest).T], axis=0)
+        correlation = section("nrcskt,cku->nrstu", stage_h, t_last)
+        scores = correlation / (box_rms[:, None] * math.sqrt(float(TMPL**3)))
+        return jnp.max(scores, axis=(2, 3, 4))[:, 0]
+
+    values = lax.map(one, spectra_kj)
+    return values.T
+
+
 def per_device(tomogram, templates, corner_z, corner_y, corner_x, loads):
     own_total = corner_z.shape[1]
     live_count = jnp.sum(loads[0, 0])
-    width = tomogram.shape[2]
-
-    def rows_of(cz, cy):
-        return lax.dynamic_slice(tomogram, (cz, cy, 0), (BOX, BOX, width))
-
-    rows = jax.vmap(rows_of)(corner_z[0], corner_y[0])
-    t_last = window_table(corner_x[0], width)
-    stage_one = jnp.einsum("nabx,nxck->ncabk", rows, t_last, preferred_element_type=jnp.float32)
-    box_spectra = forward_tail(stage_one)
-    box_rms = window_rms(rows, corner_x[0])
+    q2, box_rms = front(tomogram, corner_z[0], corner_y[0], corner_x[0])
+    real_v, imag_v = box_spectra_of(q2)
 
     all_templates = lax.all_gather(templates, "orient", axis=0, tiled=True)
     spectra = template_spectra(all_templates.reshape(-1, TMPL, TMPL, TMPL))
-    values = match(box_spectra, box_rms, spectra)
+    values = match_kj(real_v, imag_v, box_rms, spectra)
     live = jnp.arange(own_total, dtype=jnp.int32) < live_count
     matched = jnp.where(live[:, None], values, 0.0)
     return (matched[None], jnp.max(matched, axis=1)[None])

time: 462 us -> 369 us (0.80)
  matrix products: 202 us -> 69.1 us
  local copies, waits for them, and re-layouts: 161 us -> 32.6 us
  Pallas kernels: 0 us -> 124 us
  other arithmetic: 87.3 us -> 134 us
    pallas_call x0 -> x1, Pallas kernels: none -> 124 us  [front(): pl.pallas_call(front_kernel, grid_spec=grid_spec, out_shape=[jax.ShapeDty...]
    gather x45 -> x0, local copies, waits for them, and re-layouts: 92.2 us -> none
    dot_general x17 -> x15, matrix products: 123 us -> 49 us  [section(): jnp.einsum(pattern, bf(operand), table, preferred_element_type=jnp.float32)]
    convert_element_type x17 -> x20, other arithmetic: 1.94 us -> 73.6 us  [bf(): return x.astype(jnp.bfloat16)]
    another operation x4 -> x1, other arithmetic: 71.5 us -> 1.04 us  [window_table(): return jnp.stack([cos_t, sin_t], axis=2)]
    dot_general x4 -> x1, matrix products: 78.8 us -> 20.1 us  [box_spectra_of(): m3 = jnp.einsum('nzkq,wz->nwkq', q2, l3, preferred_element_type=jnp.float32)]
    convert_element_type x3 -> x2, local copies, waits for them, and re-layouts: 61 us -> 18 us  [bf(): return x.astype(jnp.bfloat16)]
    sub x0 -> x2, other arithmetic: none -> 41.1 us  [the longest x1 40.4 us: box_spectra_of(): imag = top[..., BOX:] - bottom[..., :BOX]]
where the time goes in v2:
time: 369 us; the launch traced here: 368 us
  other arithmetic  134 us (36%)
  Pallas kernels  124 us (34%)
  matrix products  69.1 us (19%)
  local copies, waits for them, and re-layouts  32.6 us (9%)
  blocking collectives  7.21 us (2%)
    pallas_call x1, Pallas kernels, front(): pl.pallas_call(front_kernel, grid_spec=grid_spec, out_shape=[jax.ShapeDty...  124 us
    convert_element_type x20, other arithmetic, bf(): return x.astype(jnp.bfloat16)  73.6 us
    dot_general x15, matrix products, section(): jnp.einsum(pattern, bf(operand), table, preferred_element_type=jnp.float32)  49 us
    sub x1, other arithmetic, box_spectra_of(): imag = top[..., BOX:] - bottom[..., :BOX]  40.4 us
    dot_general x1, matrix products, box_spectra_of(): m3 = jnp.einsum('nzkq,wz->nwkq', q2, l3, preferred_element_type=jnp.float32)  20.1 us
    convert_element_type x2, local copies, waits for them, and re-layouts, bf(): return x.astype(jnp.bfloat16)  18 us

profile of v2, /device:TPU:0, one launch (start us, length us, event | category | flops | bytes accessed | tf_op | source)
XLA Modules:
  0.0 368.1 jit_solution(674340374949294881)
XLA Ops:
  0.6 0.7 broadcast_add_fusion
  1.9 0.7 iota_subtract_fusion
  2.6 0.7 compare_and_fusion
  3.3 4.2 %fusion.84 = (bf16[15,256,1,64]{1,3,2,0:T(8,128)(2,1)S(1)}, bf16[15,256,1,64]{1,3,2,0:T(8,128)(2,1)S(1)}) fusion(s32[15,256]{1,0:T(8,128)S(1)} %iota_subtract_fusion, pred[15,256]{1,0:T(8,128)(4,1)S(1)} %compare_and_fusion), kind=kLoop, calls=%fused_computation.133 | loop fusion | flops 5160960 | bytes 1002240 | tf_op jit(solution)/shard_map/jit(_where)/select_n | solution.py:82
  7.5 1.0 pad_maximum_fusion
  8.6 1.6 copy.33.t1_ref
  10.2 0.7 iota_subtract_fusion.1
  11.0 0.7 compare_and_fusion.1
  11.7 4.7 %fusion.87 = (bf16[15,128,64]{2,1,0:T(8,128)(2,1)S(1)}, bf16[15,128,64]{2,1,0:T(8,128)(2,1)S(1)}) fusion(s32[15,128]{1,0:T(8,128)S(1)} %iota_subtract_fusion.1, pred[15,128]{1,0:T(8,128)(4,1)S(1)} %compare_and_fusion.1), kind=kLoop, calls=%fused_computation.136 | loop fusion | flops 2211840 | bytes 501120 | tf_op jit(solution)/shard_map/jit(_where)/select_n | solution.py:210
  16.7 124.5 %shard_map.77 = (bf16[15,64,64,128]{3,2,1,0:T(8,128)(2,1)}, f32[15,64,8]{2,1,0:T(8,128)S(1)}) custom-call(s32[15]{0:T(128)S(1)} %bitcast.217, bf16[80,128,256]{2,1,0:T(8,128)(2,1)} %slab_ref.1, bf16[15,256,128]{2,1,0:T(8,128)(2,1)S(1)} %copy.33.t1_ref, bf16[15,128,128]{2,1,0:T(8,128)(2,1)S(1)} %pad_maximum_fusion.1.l2_ref, ...), custom_call_target="tpu_custom_call" | custom-call | tf_op jit(solution)/shard_map/pallas_call | solution.py:237
  141.3 20.1 %fusion.54 = f32[15,66,64,128]{3,1,2,0:T(8,128)} fusion(bf16[15,64,64,128]{3,2,1,0:T(8,128)(2,1)} %get-tuple-element.105, bf16[33,64]{0,1:T(8,128)(2,1)S(1)} %get-tuple-element.172, bf16[33,64]{0,1:T(8,128)(2,1)S(1)} %get-tuple-element.173), kind=kOutput, calls=%fused_computation.88 | convolution fusion | flops 1038107136 | bytes 48177408 | tf_op jit(solution)/shard_map/nzkq,wz->nwkq/dot_general | solution.py:253
  161.4 40.4 %slice_subtract_fusion = (f32[15,33,64,64]{3,1,2,0:T(8,128)}, f32[15,33,64,64]{3,1,2,0:T(8,128)}) fusion(f32[15,66,64,128]{3,1,2,0:T(8,128)} %fusion.54), kind=kLoop, calls=%fused_computation.84 | loop fusion | flops 4055040 | bytes 48660480 | tf_op jit(solution)/shard_map/sub | solution.py:257
  202.4 7.2 %all_gather.3 = bf16[4,32,1024]{2,1,0:T(8,128)(2,1)S(1)} all-gather(bf16[1,32,1024]{2,1,0:T(8,128)(2,1)S(1)} %copy-done.1), channel_id=1, replica_groups=mesh['vol'=8,'orient'=4] {'orient'}, dimensions={0}, use_global_device_ids=true | all-gather | bytes 327680 | tf_op jit(solution)/shard_map/all_gather | solution.py:295
  210.0 2.1 reshape.1087
  212.3 2.4 convert_bitcast_fusion
  214.6 7.0 %copy.31 = bf16[4,2,32,32,64]{3,2,1,4,0:T(8,128)(2,1)} copy(bf16[4,2,32,32,64]{4,3,2,0,1:T(8,128)(2,1)S(1)} %convert_bitcast_fusion) | data formatting | bytes 2097152 | tf_op jit(solution)/shard_map/convert_element_type | solution.py:36
  221.8 5.4 %fusion.58 = bf16[4,2,32,64,64]{3,2,4,0,1:T(8,128)(2,1)} fusion(bf16[4,2,32,32,64]{3,2,1,4,0:T(8,128)(2,1)} %copy.31, bf16[1,32,2,64]{3,1,2,0:T(8,128)(2,1)S(1)} %get-tuple-element.161, bf16[1,32,2,64]{3,1,2,0:T(8,128)(2,1)S(1)} %get-tuple-element.160), kind=kOutput, calls=%fused_computation.92 | convolution fusion | flops 135274496 | bytes 3162112 | tf_op jit(solution)/shard_map/ncayk,cydj->ndajk/dot_general | solution.py:48
  227.3 11.0 %copy.32 = bf16[4,2,32,64,64]{4,2,1,3,0:T(8,128)(2,1)} copy(bf16[4,2,32,64,64]{3,2,4,0,1:T(8,128)(2,1)} %fusion.58) | data formatting | bytes 4194304 | tf_op jit(solution)/shard_map/convert_element_type | solution.py:36
  238.4 6.1 %fusion.57 = bf16[4,2,33,64,64]{3,2,4,0,1:T(8,128)(2,1)} fusion(bf16[4,2,32,64,64]{4,2,1,3,0:T(8,128)(2,1)} %copy.32, bf16[1,32,2,33]{3,1,0,2:T(8,128)(2,1)S(1)} %get-tuple-element.159, bf16[1,32,2,33]{3,1,0,2:T(8,128)(2,1)S(1)} %get-tuple-element.158), kind=kOutput, calls=%fused_computation.91 | convolution fusion | flops 139510272 | bytes 4268288 | tf_op jit(solution)/shard_map/ncajk,cadh->ndhjk/dot_general | solution.py:48
  244.5 121.2 %while.14 = (s32[]{:T(128)}, f32[4,15]{1,0:T(4,128)S(1)}, bf16[4,2,33,64,64]{3,2,4,0,1:T(8,128)(2,1)}, f32[15,33,64,64]{3,1,2,0:T(8,128)}, f32[15,33,64,64]{3,1,2,0:T(8,128)}, /*index=5*/f32[15,8,8,8]{0,3,2,1:T(8,128)S(1)}) while((s32[]{:T(128)}, f32[4,15]{1,0:T(4,128)S(1)}, bf16[4,2,33,64,64]{3,2,4,0,1:T(8,128)(2,1)}, ...), condition=%wide.region_5.6_spmd.clone, body=%wide.region_3.5_spmd.sunk.clone | while | flops 197085936 | bytes 41787484 | solution.py:285
  244.5 1.4 constant_dynamic-slice_fusion.4
  245.9 0.6 copy.82
  246.5 0.6 copy.83
  247.3 17.9 %fusion.139 = (bf16[15,1,1,33,64,64]{5,3,2,4,0,1:T(8,128)(2,1)S(1)}, bf16[15,1,1,33,64,64]{5,3,2,4,0,1:T(8,128)(2,1)}) fusion(f32[15,33,64,64]{3,1,2,0:T(8,128)} %get-tuple-element.285, f32[15,33,64,64]{3,1,2,0:T(8,128)} %get-tuple-element.284, f32[33,64,64]{2,0,1:T(8,128)S(1)} %get-tuple-element.248, f32[33,64,64]{2,0,1:T(8,128)S(1)} %get-tuple-element.249), kind=kLoop, calls=%fused_computation.7.clone.1.clone | loop fusion | flops 16220160 | bytes 25411584 | tf_op jit(solution)/shard_map/while/body/eval_jaxpr/convert_element_type | solution.py:36
  265.5 6.4 %fusion.141 = bf16[15,2,8,64,64]{4,2,3,0,1:T(8,128)(2,1)S(1)} fusion(bf16[15,1,1,33,64,64]{5,3,2,4,0,1:T(8,128)(2,1)} %get-tuple-element.250, bf16[15,1,1,33,64,64]{5,3,2,4,0,1:T(8,128)(2,1)S(1)} %get-tuple-element.251, bf16[1,33,2,8]{1,3,0,2:T(8,128)(2,1)S(1)} %get-tuple-element.254, bf16[1,33,2,8]{1,3,0,2:T(8,128)(2,1)S(1)} %get-tuple-element.255), kind=kOutput, calls=%fused_computation.13.clone.1.clone | convolution fusion | flops 146968704 | bytes 10078272 | tf_op jit(solution)/shard_map/while/body/eval_jaxpr/nrchkj,chds->nrdskj/dot_general | solution.py:48
  272.1 1.6 fusion.142
  274.0 0.8 fusion.144
  274.8 1.4 constant_dynamic-slice_fusion.4
  276.8 0.6 copy.83
  277.6 17.9 %fusion.139 = (bf16[15,1,1,33,64,64]{5,3,2,4,0,1:T(8,128)(2,1)S(1)}, bf16[15,1,1,33,64,64]{5,3,2,4,0,1:T(8,128)(2,1)}) fusion(f32[15,33,64,64]{3,1,2,0:T(8,128)} %get-tuple-element.285, f32[15,33,64,64]{3,1,2,0:T(8,128)} %get-tuple-element.284, f32[33,64,64]{2,0,1:T(8,128)S(1)} %get-tuple-element.248, f32[33,64,64]{2,0,1:T(8,128)S(1)} %get-tuple-element.249), kind=kLoop, calls=%fused_computation.7.clone.1.clone | loop fusion | flops 16220160 | bytes 25411584 | tf_op jit(solution)/shard_map/while/body/eval_jaxpr/convert_element_type | solution.py:36
  295.8 6.4 %fusion.141 = bf16[15,2,8,64,64]{4,2,3,0,1:T(8,128)(2,1)S(1)} fusion(bf16[15,1,1,33,64,64]{5,3,2,4,0,1:T(8,128)(2,1)} %get-tuple-element.250, bf16[15,1,1,33,64,64]{5,3,2,4,0,1:T(8,128)(2,1)S(1)} %get-tuple-element.251, bf16[1,33,2,8]{1,3,0,2:T(8,128)(2,1)S(1)} %get-tuple-element.254, bf16[1,33,2,8]{1,3,0,2:T(8,128)(2,1)S(1)} %get-tuple-element.255), kind=kOutput, calls=%fused_computation.13.clone.1.clone | convolution fusion | flops 146968704 | bytes 10078272 | tf_op jit(solution)/shard_map/while/body/eval_jaxpr/nrchkj,chds->nrdskj/dot_general | solution.py:48
  302.4 1.6 fusion.142
  304.3 0.8 fusion.144
  305.1 1.4 constant_dynamic-slice_fusion.4
  306.5 0.6 copy.82
  307.9 17.9 %fusion.139 = (bf16[15,1,1,33,64,64]{5,3,2,4,0,1:T(8,128)(2,1)S(1)}, bf16[15,1,1,33,64,64]{5,3,2,4,0,1:T(8,128)(2,1)}) fusion(f32[15,33,64,64]{3,1,2,0:T(8,128)} %get-tuple-element.285, f32[15,33,64,64]{3,1,2,0:T(8,128)} %get-tuple-element.284, f32[33,64,64]{2,0,1:T(8,128)S(1)} %get-tuple-element.248, f32[33,64,64]{2,0,1:T(8,128)S(1)} %get-tuple-element.249), kind=kLoop, calls=%fused_computation.7.clone.1.clone | loop fusion | flops 16220160 | bytes 25411584 | tf_op jit(solution)/shard_map/while/body/eval_jaxpr/convert_element_type | solution.py:36
  326.1 6.4 %fusion.141 = bf16[15,2,8,64,64]{4,2,3,0,1:T(8,128)(2,1)S(1)} fusion(bf16[15,1,1,33,64,64]{5,3,2,4,0,1:T(8,128)(2,1)} %get-tuple-element.250, bf16[15,1,1,33,64,64]{5,3,2,4,0,1:T(8,128)(2,1)S(1)} %get-tuple-element.251, bf16[1,33,2,8]{1,3,0,2:T(8,128)(2,1)S(1)} %get-tuple-element.254, bf16[1,33,2,8]{1,3,0,2:T(8,128)(2,1)S(1)} %get-tuple-element.255), kind=kOutput, calls=%fused_computation.13.clone.1.clone | convolution fusion | flops 146968704 | bytes 10078272 | tf_op jit(solution)/shard_map/while/body/eval_jaxpr/nrchkj,chds->nrdskj/dot_general | solution.py:48
  332.7 1.6 fusion.142
  334.6 0.8 fusion.144
  335.4 1.4 constant_dynamic-slice_fusion.4
  337.4 0.6 copy.83
  338.2 17.9 %fusion.139 = (bf16[15,1,1,33,64,64]{5,3,2,4,0,1:T(8,128)(2,1)S(1)}, bf16[15,1,1,33,64,64]{5,3,2,4,0,1:T(8,128)(2,1)}) fusion(f32[15,33,64,64]{3,1,2,0:T(8,128)} %get-tuple-element.285, f32[15,33,64,64]{3,1,2,0:T(8,128)} %get-tuple-element.284, f32[33,64,64]{2,0,1:T(8,128)S(1)} %get-tuple-element.248, f32[33,64,64]{2,0,1:T(8,128)S(1)} %get-tuple-element.249), kind=kLoop, calls=%fused_computation.7.clone.1.clone | loop fusion | flops 16220160 | bytes 25411584 | tf_op jit(solution)/shard_map/while/body/eval_jaxpr/convert_element_type | solution.py:36
  356.4 6.4 %fusion.141 = bf16[15,2,8,64,64]{4,2,3,0,1:T(8,128)(2,1)S(1)} fusion(bf16[15,1,1,33,64,64]{5,3,2,4,0,1:T(8,128)(2,1)} %get-tuple-element.250, bf16[15,1,1,33,64,64]{5,3,2,4,0,1:T(8,128)(2,1)S(1)} %get-tuple-element.251, bf16[1,33,2,8]{1,3,0,2:T(8,128)(2,1)S(1)} %get-tuple-element.254, bf16[1,33,2,8]{1,3,0,2:T(8,128)(2,1)S(1)} %get-tuple-element.255), kind=kOutput, calls=%fused_computation.13.clone.1.clone | convolution fusion | flops 146968704 | bytes 10078272 | tf_op jit(solution)/shard_map/while/body/eval_jaxpr/nrchkj,chds->nrdskj/dot_general | solution.py:48
  363.0 1.6 fusion.142
  364.9 0.8 fusion.144
  365.7 0.6 reduce_sum.27
  366.4 0.6 iota_compare_fusion.4
  367.0 1.1 select_reduce_fusion
  (77 shorter events, 8.1 us)
Async XLA Ops:
  0.6 16.0 %copy-start = (s32[1,15]{1,0:T(1,128)S(1)}, s32[1,15]{1,0:T(1,128)}, u32[]{:S(2)}) copy-start(s32[1,15]{1,0:T(1,128)} %param.10) | copy-start | bytes 184
  161.4 41.0 %copy-start.1 = (bf16[1,32,1024]{2,1,0:T(8,128)(2,1)S(1)}, bf16[1,32,1024]{2,1,0:T(8,128)(2,1)}, u32[]{:S(2)}) copy-start(bf16[1,32,1024]{2,1,0:T(8,128)(2,1)} %param.9) | copy-start | bytes 196612
  244.5 121.2 %copy-start.2 = (s32[1,1,8]{2,1,0:T(1,128)S(1)}, s32[1,1,8]{2,1,0:T(1,128)}, u32[]{:S(2)}) copy-start(s32[1,1,8]{2,1,0:T(1,128)} %param.13) | copy-start | bytes 100

commit v3 on v2

--- a/solution.py
+++ b/solution.py
@@ -154,8 +154,10 @@
         part_b = m2[:, 1]
         lane = lax.broadcasted_iota(jnp.int32, part_a.shape, 2)
         sign = jnp.where(lane < BOX, 1.0, -1.0).astype(jnp.float32)
-        out = pltpu.roll(part_b, BOX, 2) + sign * part_a
-        q2_ref[pl.ds(z0, chunk)] = out.astype(jnp.bfloat16)
+        out = (pltpu.roll(part_b, BOX, 2) + sign * part_a).astype(jnp.bfloat16).astype(jnp.float32)
+        q2_ref[0, pl.ds(z0, chunk)] = out.astype(jnp.bfloat16)
+        swapped = sign * pltpu.roll(out, BOX, 2)
+        q2_ref[1, pl.ds(z0, chunk)] = swapped.astype(jnp.bfloat16)
         return carry
 
     lax.fori_loop(0, depth // chunk, transform_chunk, 0)
@@ -226,7 +228,7 @@
             pl.BlockSpec((None, width, SHIFT), lambda n, cz: (n, 0, 0)),
         ],
         out_specs=[
-            pl.BlockSpec((None, BOX, BOX, 2 * BOX), lambda n, cz: (n, 0, 0, 0)),
+            pl.BlockSpec((None, 2, BOX, BOX, 2 * BOX), lambda n, cz: (n, 0, 0, 0, 0)),
             pl.BlockSpec((None, SHIFT * SHIFT, SHIFT), lambda n, cz: (n, 0, 0)),
         ],
         scratch_shapes=[
@@ -238,7 +240,7 @@
         front_kernel,
         grid_spec=grid_spec,
         out_shape=[
-            jax.ShapeDtypeStruct((count, BOX, BOX, 2 * BOX), jnp.bfloat16),
+            jax.ShapeDtypeStruct((count, 2, BOX, BOX, 2 * BOX), jnp.bfloat16),
             jax.ShapeDtypeStruct((count, SHIFT * SHIFT, SHIFT), jnp.float32),
         ],
         compiler_params=pltpu.CompilerParams(vmem_limit_bytes=48 * 1024 * 1024),
@@ -249,17 +251,14 @@
 
 def box_spectra_of(q2):
     cos_half, sin_half = phases(HALF, BOX, 0)
-    l3 = jnp.concatenate([bf(cos_half), bf(sin_half)], axis=0)
-    m3 = jnp.einsum("nzkq,wz->nwkq", q2, l3, preferred_element_type=jnp.float32)
-    top = m3[:, :HALF]
-    bottom = m3[:, HALF:]
-    real = top[..., :BOX] + bottom[..., BOX:]
-    imag = top[..., BOX:] - bottom[..., :BOX]
-    return real, imag
-
-
-def match_kj(real_v, imag_v, box_rms, spectra):
+    l3 = jnp.stack([bf(cos_half).T, bf(sin_half).T], axis=0)
+    return jnp.einsum("nwzkq,wzh->nhkq", q2, l3, preferred_element_type=jnp.float32)
+
+
+def match_kj(spectrum_v, box_rms, spectra):
     spectra_kj = jnp.swapaxes(spectra, 3, 4)
+    real_v = spectrum_v[..., :BOX]
+    imag_v = spectrum_v[..., BOX:]
 
     def one(spectrum):
         real_t = spectrum[0].astype(jnp.float32)[None, None]
@@ -290,11 +289,11 @@
     own_total = corner_z.shape[1]
     live_count = jnp.sum(loads[0, 0])
     q2, box_rms = front(tomogram, corner_z[0], corner_y[0], corner_x[0])
-    real_v, imag_v = box_spectra_of(q2)
+    spectrum_v = box_spectra_of(q2)
 
     all_templates = lax.all_gather(templates, "orient", axis=0, tiled=True)
     spectra = template_spectra(all_templates.reshape(-1, TMPL, TMPL, TMPL))
-    values = match_kj(real_v, imag_v, box_rms, spectra)
+    values = match_kj(spectrum_v, box_rms, spectra)
     live = jnp.arange(own_total, dtype=jnp.int32) < live_count
     matched = jnp.where(live[:, None], values, 0.0)
     return (matched[None], jnp.max(matched, axis=1)[None])

time: 369 us -> 378 us (1.024)
  other arithmetic: 134 us -> 91.8 us
  local copies, waits for them, and re-layouts: 32.6 us -> 62.3 us
  matrix products: 69.1 us -> 81.9 us
  Pallas kernels: 124 us -> 133 us
    sub x1 -> x0, other arithmetic: 40.4 us -> none  [box_spectra_of(): imag = top[..., BOX:] - bottom[..., :BOX]]
    slice x0 -> x1, local copies, waits for them, and re-layouts: none -> 30 us  [match_kj(): imag_v = spectrum_v[..., BOX:]]
    dot_general x1, matrix products: 20.1 us -> 32.9 us  [box_spectra_of(): jnp.einsum('nwzkq,wzh->nhkq', q2, l3, preferred_element_type=jnp.float32)]
    pallas_call x1, Pallas kernels: 124 us -> 133 us  [front(): pl.pallas_call(front_kernel, grid_spec=grid_spec, out_shape=[jax.ShapeDty...]
where the time goes in v3:
time: 378 us
  Pallas kernels  133 us (35%)
  other arithmetic  91.8 us (24%)
  matrix products  81.9 us (22%)
  local copies, waits for them, and re-layouts  62.3 us (16%)
  blocking collectives  7.22 us (2%)
    pallas_call x1, Pallas kernels, front(): pl.pallas_call(front_kernel, grid_spec=grid_spec, out_shape=[jax.ShapeDty...  133 us
    convert_element_type x20, other arithmetic, bf(): return x.astype(jnp.bfloat16)  73.3 us
    dot_general x15, matrix products, section(): jnp.einsum(pattern, bf(operand), table, preferred_element_type=jnp.float32)  49 us
    dot_general x1, matrix products, box_spectra_of(): jnp.einsum('nwzkq,wzh->nhkq', q2, l3, preferred_element_type=jnp.float32)  32.9 us
    slice x1, local copies, waits for them, and re-layouts, match_kj(): imag_v = spectrum_v[..., BOX:]  30 us
    convert_element_type x2, local copies, waits for them, and re-layouts, bf(): return x.astype(jnp.bfloat16)  17.7 us

profile of v3, /device:TPU:0, one launch (start us, length us, event | category | flops | bytes accessed | tf_op | source)
XLA Modules:
  0.0 377.5 jit_solution(4748058038659914059)
XLA Ops:
  0.7 0.8 broadcast_add_fusion
  1.9 0.7 iota_subtract_fusion
  2.6 0.7 compare_and_fusion
  3.4 4.2 %fusion.84 = (bf16[15,256,1,64]{1,3,2,0:T(8,128)(2,1)S(1)}, bf16[15,256,1,64]{1,3,2,0:T(8,128)(2,1)S(1)}) fusion(s32[15,256]{1,0:T(8,128)S(1)} %iota_subtract_fusion, pred[15,256]{1,0:T(8,128)(4,1)S(1)} %compare_and_fusion), kind=kLoop, calls=%fused_computation.131 | loop fusion | flops 5160960 | bytes 1002240 | tf_op jit(solution)/shard_map/jit(_where)/select_n | solution.py:82
  7.6 1.0 pad_maximum_fusion
  8.6 1.6 copy.33.t1_ref
  10.4 4.7 %fusion.87 = (bf16[15,128,64]{2,1,0:T(8,128)(2,1)S(1)}, bf16[15,128,64]{2,1,0:T(8,128)(2,1)S(1)}) fusion(s32[15,128]{1,0:T(8,128)S(1)} %iota_subtract_fusion.1, pred[15,128]{1,0:T(8,128)(4,1)S(1)} %compare_and_fusion.1), kind=kLoop, calls=%fused_computation.134 | loop fusion | flops 2211840 | bytes 501120 | tf_op jit(solution)/shard_map/jit(_where)/select_n | solution.py:212
  15.4 133.2 %shard_map.77 = (bf16[15,2,64,64,128]{4,3,2,1,0:T(8,128)(2,1)}, f32[15,64,8]{2,1,0:T(8,128)S(1)}) custom-call(s32[15]{0:T(128)S(1)} %bitcast.220, bf16[80,128,256]{2,1,0:T(8,128)(2,1)} %slab_ref.1, bf16[15,256,128]{2,1,0:T(8,128)(2,1)S(1)} %copy.33.t1_ref, bf16[15,128,128]{2,1,0:T(8,128)(2,1)S(1)} %pad_maximum_fusion.1.l2_ref, ...), custom_call_target="tpu_custom_call" | custom-call | tf_op jit(solution)/shard_map/pallas_call | solution.py:239
  148.7 32.9 %fusion.54 = f32[15,33,64,128]{3,1,2,0:T(8,128)} fusion(bf16[15,2,64,64,128]{4,3,2,1,0:T(8,128)(2,1)} %get-tuple-element.105, bf16[1,64,33]{1,2,0:T(8,128)(2,1)S(1)} %get-tuple-element.172, bf16[1,64,33]{1,2,0:T(8,128)(2,1)S(1)} %get-tuple-element.173), kind=kOutput, calls=%fused_computation.88 | convolution fusion | flops 1038107136 | bytes 47685888 | tf_op jit(solution)/shard_map/nwzkq,wzh->nhkq/dot_general | solution.py:255
  181.7 30.0 %fusion.121 = (f32[15,33,64,64]{3,1,2,0:T(8,128)}, f32[15,33,64,64]{3,1,2,0:T(8,128)}) fusion(f32[15,33,64,128]{3,1,2,0:T(8,128)} %fusion.54), kind=kLoop, calls=%fused_computation.208 | loop fusion | bytes 32440320 | tf_op jit(solution)/shard_map/slice | solution.py:261
  212.3 7.2 %all_gather.3 = bf16[4,32,1024]{2,1,0:T(8,128)(2,1)S(1)} all-gather(bf16[1,32,1024]{2,1,0:T(8,128)(2,1)S(1)} %copy-done.1), channel_id=1, replica_groups=mesh['vol'=8,'orient'=4] {'orient'}, dimensions={0}, use_global_device_ids=true | all-gather | bytes 327680 | tf_op jit(solution)/shard_map/all_gather | solution.py:294
  219.9 2.0 reshape.1161
  222.1 2.4 convert_bitcast_fusion
  224.5 6.8 %copy.31 = bf16[4,2,32,32,64]{3,2,1,4,0:T(8,128)(2,1)} copy(bf16[4,2,32,32,64]{4,3,2,0,1:T(8,128)(2,1)S(1)} %convert_bitcast_fusion) | data formatting | bytes 2097152 | tf_op jit(solution)/shard_map/convert_element_type | solution.py:36
  231.5 5.5 %fusion.58 = bf16[4,2,32,64,64]{3,2,4,0,1:T(8,128)(2,1)} fusion(bf16[4,2,32,32,64]{3,2,1,4,0:T(8,128)(2,1)} %copy.31, bf16[1,32,2,64]{3,1,2,0:T(8,128)(2,1)S(1)} %get-tuple-element.161, bf16[1,32,2,64]{3,1,2,0:T(8,128)(2,1)S(1)} %get-tuple-element.160), kind=kOutput, calls=%fused_computation.90 | convolution fusion | flops 135274496 | bytes 3162112 | tf_op jit(solution)/shard_map/ncayk,cydj->ndajk/dot_general | solution.py:48
  236.9 10.9 %copy.32 = bf16[4,2,32,64,64]{4,2,1,3,0:T(8,128)(2,1)} copy(bf16[4,2,32,64,64]{3,2,4,0,1:T(8,128)(2,1)} %fusion.58) | data formatting | bytes 4194304 | tf_op jit(solution)/shard_map/convert_element_type | solution.py:36
  248.1 6.1 %fusion.57 = bf16[4,2,33,64,64]{3,2,4,0,1:T(8,128)(2,1)} fusion(bf16[4,2,32,64,64]{4,2,1,3,0:T(8,128)(2,1)} %copy.32, bf16[1,32,2,33]{3,1,0,2:T(8,128)(2,1)S(1)} %get-tuple-element.159, bf16[1,32,2,33]{3,1,0,2:T(8,128)(2,1)S(1)} %get-tuple-element.158), kind=kOutput, calls=%fused_computation.89 | convolution fusion | flops 139510272 | bytes 4268288 | tf_op jit(solution)/shard_map/ncajk,cadh->ndhjk/dot_general | solution.py:48
  254.1 121.0 %while.14 = (s32[]{:T(128)}, f32[4,15]{1,0:T(4,128)S(1)}, bf16[4,2,33,64,64]{3,2,4,0,1:T(8,128)(2,1)}, f32[15,33,64,64]{3,1,2,0:T(8,128)}, f32[15,33,64,64]{3,1,2,0:T(8,128)}, /*index=5*/f32[15,8,8,8]{0,3,2,1:T(8,128)S(1)}) while((s32[]{:T(128)}, f32[4,15]{1,0:T(4,128)S(1)}, bf16[4,2,33,64,64]{3,2,4,0,1:T(8,128)(2,1)}, ...), condition=%wide.region_5.6_spmd.clone, body=%wide.region_3.5_spmd.sunk.clone | while | flops 197085936 | bytes 41787484 | solution.py:284
  254.1 1.4 constant_dynamic-slice_fusion.4
  255.6 0.6 copy.83
  256.2 0.6 copy.84
  256.9 17.9 %fusion.140 = (bf16[15,1,1,33,64,64]{5,3,2,4,0,1:T(8,128)(2,1)S(1)}, bf16[15,1,1,33,64,64]{5,3,2,4,0,1:T(8,128)(2,1)}) fusion(f32[15,33,64,64]{3,1,2,0:T(8,128)} %get-tuple-element.285, f32[15,33,64,64]{3,1,2,0:T(8,128)} %get-tuple-element.284, f32[33,64,64]{2,0,1:T(8,128)S(1)} %get-tuple-element.248, f32[33,64,64]{2,0,1:T(8,128)S(1)} %get-tuple-element.249), kind=kLoop, calls=%fused_computation.7.clone.1.clone | loop fusion | flops 16220160 | bytes 25411584 | tf_op jit(solution)/shard_map/while/body/eval_jaxpr/convert_element_type | solution.py:36
  275.1 6.4 %fusion.142 = bf16[15,2,8,64,64]{4,2,3,0,1:T(8,128)(2,1)S(1)} fusion(bf16[15,1,1,33,64,64]{5,3,2,4,0,1:T(8,128)(2,1)} %get-tuple-element.250, bf16[15,1,1,33,64,64]{5,3,2,4,0,1:T(8,128)(2,1)S(1)} %get-tuple-element.251, bf16[1,33,2,8]{1,3,0,2:T(8,128)(2,1)S(1)} %get-tuple-element.254, bf16[1,33,2,8]{1,3,0,2:T(8,128)(2,1)S(1)} %get-tuple-element.255), kind=kOutput, calls=%fused_computation.13.clone.1.clone | convolution fusion | flops 146968704 | bytes 10078272 | tf_op jit(solution)/shard_map/while/body/eval_jaxpr/nrchkj,chds->nrdskj/dot_general | solution.py:48
  281.7 1.6 fusion.143
  283.6 0.8 fusion.145
  284.4 1.4 constant_dynamic-slice_fusion.4
  286.4 0.6 copy.84
  287.2 17.9 %fusion.140 = (bf16[15,1,1,33,64,64]{5,3,2,4,0,1:T(8,128)(2,1)S(1)}, bf16[15,1,1,33,64,64]{5,3,2,4,0,1:T(8,128)(2,1)}) fusion(f32[15,33,64,64]{3,1,2,0:T(8,128)} %get-tuple-element.285, f32[15,33,64,64]{3,1,2,0:T(8,128)} %get-tuple-element.284, f32[33,64,64]{2,0,1:T(8,128)S(1)} %get-tuple-element.248, f32[33,64,64]{2,0,1:T(8,128)S(1)} %get-tuple-element.249), kind=kLoop, calls=%fused_computation.7.clone.1.clone | loop fusion | flops 16220160 | bytes 25411584 | tf_op jit(solution)/shard_map/while/body/eval_jaxpr/convert_element_type | solution.py:36
  305.3 6.4 %fusion.142 = bf16[15,2,8,64,64]{4,2,3,0,1:T(8,128)(2,1)S(1)} fusion(bf16[15,1,1,33,64,64]{5,3,2,4,0,1:T(8,128)(2,1)} %get-tuple-element.250, bf16[15,1,1,33,64,64]{5,3,2,4,0,1:T(8,128)(2,1)S(1)} %get-tuple-element.251, bf16[1,33,2,8]{1,3,0,2:T(8,128)(2,1)S(1)} %get-tuple-element.254, bf16[1,33,2,8]{1,3,0,2:T(8,128)(2,1)S(1)} %get-tuple-element.255), kind=kOutput, calls=%fused_computation.13.clone.1.clone | convolution fusion | flops 146968704 | bytes 10078272 | tf_op jit(solution)/shard_map/while/body/eval_jaxpr/nrchkj,chds->nrdskj/dot_general | solution.py:48
  312.0 1.6 fusion.143
  313.8 0.8 fusion.145
  314.7 1.4 constant_dynamic-slice_fusion.4
  316.1 0.6 copy.83
  316.7 0.6 copy.84
  317.4 17.9 %fusion.140 = (bf16[15,1,1,33,64,64]{5,3,2,4,0,1:T(8,128)(2,1)S(1)}, bf16[15,1,1,33,64,64]{5,3,2,4,0,1:T(8,128)(2,1)}) fusion(f32[15,33,64,64]{3,1,2,0:T(8,128)} %get-tuple-element.285, f32[15,33,64,64]{3,1,2,0:T(8,128)} %get-tuple-element.284, f32[33,64,64]{2,0,1:T(8,128)S(1)} %get-tuple-element.248, f32[33,64,64]{2,0,1:T(8,128)S(1)} %get-tuple-element.249), kind=kLoop, calls=%fused_computation.7.clone.1.clone | loop fusion | flops 16220160 | bytes 25411584 | tf_op jit(solution)/shard_map/while/body/eval_jaxpr/convert_element_type | solution.py:36
  335.6 6.4 %fusion.142 = bf16[15,2,8,64,64]{4,2,3,0,1:T(8,128)(2,1)S(1)} fusion(bf16[15,1,1,33,64,64]{5,3,2,4,0,1:T(8,128)(2,1)} %get-tuple-element.250, bf16[15,1,1,33,64,64]{5,3,2,4,0,1:T(8,128)(2,1)S(1)} %get-tuple-element.251, bf16[1,33,2,8]{1,3,0,2:T(8,128)(2,1)S(1)} %get-tuple-element.254, bf16[1,33,2,8]{1,3,0,2:T(8,128)(2,1)S(1)} %get-tuple-element.255), kind=kOutput, calls=%fused_computation.13.clone.1.clone | convolution fusion | flops 146968704 | bytes 10078272 | tf_op jit(solution)/shard_map/while/body/eval_jaxpr/nrchkj,chds->nrdskj/dot_general | solution.py:48
  342.2 1.6 fusion.143
  344.1 0.8 fusion.145
  344.9 1.4 constant_dynamic-slice_fusion.4
  346.3 0.6 copy.83
  346.9 0.6 copy.84
  347.7 17.9 %fusion.140 = (bf16[15,1,1,33,64,64]{5,3,2,4,0,1:T(8,128)(2,1)S(1)}, bf16[15,1,1,33,64,64]{5,3,2,4,0,1:T(8,128)(2,1)}) fusion(f32[15,33,64,64]{3,1,2,0:T(8,128)} %get-tuple-element.285, f32[15,33,64,64]{3,1,2,0:T(8,128)} %get-tuple-element.284, f32[33,64,64]{2,0,1:T(8,128)S(1)} %get-tuple-element.248, f32[33,64,64]{2,0,1:T(8,128)S(1)} %get-tuple-element.249), kind=kLoop, calls=%fused_computation.7.clone.1.clone | loop fusion | flops 16220160 | bytes 25411584 | tf_op jit(solution)/shard_map/while/body/eval_jaxpr/convert_element_type | solution.py:36
  365.8 6.4 %fusion.142 = bf16[15,2,8,64,64]{4,2,3,0,1:T(8,128)(2,1)S(1)} fusion(bf16[15,1,1,33,64,64]{5,3,2,4,0,1:T(8,128)(2,1)} %get-tuple-element.250, bf16[15,1,1,33,64,64]{5,3,2,4,0,1:T(8,128)(2,1)S(1)} %get-tuple-element.251, bf16[1,33,2,8]{1,3,0,2:T(8,128)(2,1)S(1)} %get-tuple-element.254, bf16[1,33,2,8]{1,3,0,2:T(8,128)(2,1)S(1)} %get-tuple-element.255), kind=kOutput, calls=%fused_computation.13.clone.1.clone | convolution fusion | flops 146968704 | bytes 10078272 | tf_op jit(solution)/shard_map/while/body/eval_jaxpr/nrchkj,chds->nrdskj/dot_general | solution.py:48
  372.5 1.6 fusion.143
  374.3 0.8 fusion.145
  375.2 0.6 reduce_sum.27
  375.8 0.6 iota_compare_fusion.4
  376.5 1.1 select_reduce_fusion
  (79 shorter events, 7.0 us)
Async XLA Ops:
  0.6 9.6 %copy-start.2 = (s32[1,15]{1,0:T(1,128)S(1)}, s32[1,15]{1,0:T(1,128)}, u32[]{:S(2)}) copy-start(s32[1,15]{1,0:T(1,128)} %param.11) | copy-start | bytes 184
  0.6 14.7 %copy-start = (s32[1,15]{1,0:T(1,128)S(1)}, s32[1,15]{1,0:T(1,128)}, u32[]{:S(2)}) copy-start(s32[1,15]{1,0:T(1,128)} %param.10) | copy-start | bytes 184
  181.7 30.7 %copy-start.1 = (bf16[1,32,1024]{2,1,0:T(8,128)(2,1)S(1)}, bf16[1,32,1024]{2,1,0:T(8,128)(2,1)}, u32[]{:S(2)}) copy-start(bf16[1,32,1024]{2,1,0:T(8,128)(2,1)} %param.9) | copy-start | bytes 196612
  254.1 121.0 %copy-start.3 = (s32[1,1,8]{2,1,0:T(1,128)S(1)}, s32[1,1,8]{2,1,0:T(1,128)}, u32[]{:S(2)}) copy-start(s32[1,1,8]{2,1,0:T(1,128)} %param.13) | copy-start | bytes 100

commit v4 on v3

--- a/solution.py
+++ b/solution.py
@@ -256,32 +256,38 @@
 
 
 def match_kj(spectrum_v, box_rms, spectra):
-    spectra_kj = jnp.swapaxes(spectra, 3, 4)
+    count_r = spectra.shape[0]
+    spectra_kq = jnp.transpose(spectra, (0, 2, 4, 1, 3)).reshape(count_r, HALF, BOX, 2 * BOX)
     real_v = spectrum_v[..., :BOX]
     imag_v = spectrum_v[..., BOX:]
+    cos_first, sin_first = phases(SHIFT, HALF, shift_anchor())
+    freq_index = jnp.arange(HALF, dtype=jnp.int32)
+    weight = jnp.where(freq_index % (BOX // 2) == 0, 1.0, 2.0) / float(BOX**3)
+    t_first = jnp.stack([bf(cos_first * weight[None, :]).T, bf(sin_first * weight[None, :]).T], axis=0)
+    cos_rest, sin_rest = phases(SHIFT, BOX, shift_anchor())
+    c_rest = bf(cos_rest).T
+    s_rest = bf(sin_rest).T
+    t_mid = jnp.concatenate(
+        [jnp.concatenate([c_rest, s_rest], axis=1), jnp.concatenate([-s_rest, c_rest], axis=1)], axis=0
+    )
+    t_last = jnp.stack([c_rest, -s_rest], axis=0)
 
     def one(spectrum):
-        real_t = spectrum[0].astype(jnp.float32)[None, None]
-        imag_t = spectrum[1].astype(jnp.float32)[None, None]
-        rv = real_v[:, None]
-        iv = imag_v[:, None]
-        real_p = real_t * rv + imag_t * iv
-        imag_p = real_t * iv - imag_t * rv
-        cross = jnp.stack([bf(real_p), bf(imag_p)], axis=2)
-        cos_first, sin_first = phases(SHIFT, HALF, shift_anchor())
-        freq_index = jnp.arange(HALF, dtype=jnp.int32)
-        weight = jnp.where(freq_index % (BOX // 2) == 0, 1.0, 2.0) / float(BOX**3)
-        t_first = complex_table(cos_first * weight[None, :], sin_first * weight[None, :], -1.0, 1.0)
-        stage_g = section("nrchkj,chds->nrdskj", cross, t_first)
-        cos_rest, sin_rest = phases(SHIFT, BOX, shift_anchor())
-        t_mid = complex_table(cos_rest, sin_rest, -1.0, 1.0)
-        stage_h = section("nrcskj,cjdt->nrdskt", stage_g, t_mid)
-        t_last = jnp.stack([bf(cos_rest).T, -bf(sin_rest).T], axis=0)
-        correlation = section("nrcskt,cku->nrstu", stage_h, t_last)
-        scores = correlation / (box_rms[:, None] * math.sqrt(float(TMPL**3)))
-        return jnp.max(scores, axis=(2, 3, 4))[:, 0]
-
-    values = lax.map(one, spectra_kj)
+        real_t = spectrum[None, ..., :BOX].astype(jnp.float32)
+        imag_t = spectrum[None, ..., BOX:].astype(jnp.float32)
+        real_p = bf(real_t * real_v + imag_t * imag_v)
+        imag_p = bf(real_t * imag_v - imag_t * real_v)
+        plain = jnp.concatenate([real_p, imag_p], axis=-1)
+        turned = jnp.concatenate([-imag_p, real_p], axis=-1)
+        cross = jnp.stack([plain, turned], axis=1)
+        stage_g = jnp.einsum("nwhkq,whs->nskq", cross, t_first, preferred_element_type=jnp.float32)
+        stage_h = jnp.einsum("nskq,qp->nskp", bf(stage_g), t_mid, preferred_element_type=jnp.float32)
+        stage_h = bf(stage_h).reshape(stage_h.shape[0], SHIFT, BOX, 2, SHIFT)
+        correlation = jnp.einsum("nskdt,dku->nstu", stage_h, t_last, preferred_element_type=jnp.float32)
+        scores = correlation / (box_rms * math.sqrt(float(TMPL**3)))
+        return jnp.max(scores, axis=(1, 2, 3))
+
+    values = lax.map(one, spectra_kq)
     return values.T
 
 

time: 378 us -> 540 us (1.43)
  other arithmetic: 91.8 us -> 238 us
  local copies, waits for them, and re-layouts: 62.3 us -> 88.5 us
  matrix products: 81.9 us -> 70.8 us
    neg x4 -> x6, other arithmetic: 0.48 us -> 93.2 us  [the longest x4 93 us: one(): turned = jnp.concatenate([-imag_p, real_p], axis=-1)]
    another operation x0 -> x6, other arithmetic: none -> 74.9 us  [the longest x4 74.9 us: one(): cross = jnp.stack([plain, turned], axis=1)]
    dot_general x15 -> x3, matrix products: 49 us -> 13.9 us  [section(): jnp.einsum(pattern, bf(operand), table, preferred_element_type=jnp.float32)]
    while x9 -> x43, local copies, waits for them, and re-layouts: 5.13 us -> 31.8 us  [the longest x3 24.2 us: match_kj(): values = lax.map(one, spectra_kq)]
    dot_general x0 -> x12, matrix products: none -> 24 us  [the longest x4 14.3 us: one(): jnp.einsum('nwhkq,whs->nskq', cross, t_first, preferred_element_type=jnp....]
    convert_element_type x20 -> x11, other arithmetic: 73.3 us -> 50.9 us  [bf(): return x.astype(jnp.bfloat16)]
    slice x4 -> x0, local copies, waits for them, and re-layouts: 5.63 us -> none  [one(): real_t = spectrum[0].astype(jnp.float32)[None, None]]
where the time goes in v4:
time: 540 us; the launch traced here: 539 us
  other arithmetic  238 us (44%)
  Pallas kernels  133 us (25%)
  local copies, waits for them, and re-layouts  88.5 us (16%)
  matrix products  70.8 us (13%)
  blocking collectives  7.21 us (1%)
    pallas_call x1, Pallas kernels, front(): pl.pallas_call(front_kernel, grid_spec=grid_spec, out_shape=[jax.ShapeDty...  133 us
    neg x4, other arithmetic, one(): turned = jnp.concatenate([-imag_p, real_p], axis=-1)  93 us
    another operation x4, other arithmetic, one(): cross = jnp.stack([plain, turned], axis=1)  74.9 us
    convert_element_type x11, other arithmetic, bf(): return x.astype(jnp.bfloat16)  50.9 us
    dot_general x1, matrix products, box_spectra_of(): jnp.einsum('nwzkq,wzh->nhkq', q2, l3, preferred_element_type=jnp.float32)  32.9 us
    slice x1, local copies, waits for them, and re-layouts, match_kj(): imag_v = spectrum_v[..., BOX:]  30 us
    while x3, local copies, waits for them, and re-layouts, match_kj(): values = lax.map(one, spectra_kq)  24.2 us
    convert_element_type x2, local copies, waits for them, and re-layouts, bf(): return x.astype(jnp.bfloat16)  17.7 us

profile of v4, /device:TPU:0, one launch (start us, length us, event | category | flops | bytes accessed | tf_op | source)
XLA Modules:
  0.0 538.9 jit_solution(13166817996962595243)
XLA Ops:
  3.3 4.2 fusion.56
  7.5 1.0 pad_maximum_fusion
  8.6 1.6 copy.30.t1_ref
  11.6 4.7 fusion.59
  17.3 133.2 %shard_map.77 = (bf16[15,2,64,64,128]{4,3,2,1,0:T(8,128)(2,1)}, f32[15,64,8]{2,1,0:T(8,128)S(1)}) custom-call(s32[15]{0:T(128)S(1)} %bitcast.146, bf16[80,128,256]{2,1,0:T(8,128)(2,1)} %slab_ref.1, bf16[15,256,128]{2,1,0:T(8,128)(2,1)S(1)} %copy.30.t1_ref, bf16[15,128,128]{2,1,0:T(8,128)(2,1)S(1)} %pad_maximum_fusion.1.l2_ref, ...), custom_call_target="tpu_custom_call" | custom-call | tf_op jit(solution)/shard_map/pallas_call | solution.py:239
  150.6 32.9 %fusion.26 = f32[15,33,64,128]{3,1,2,0:T(8,128)} fusion(bf16[15,2,64,64,128]{4,3,2,1,0:T(8,128)(2,1)} %get-tuple-element.51, bf16[1,64,33]{1,2,0:T(8,128)(2,1)S(1)} %get-tuple-element.129, bf16[1,64,33]{1,2,0:T(8,128)(2,1)S(1)} %get-tuple-element.130), kind=kOutput, calls=%fused_computation.29 | convolution fusion | flops 1038107136 | bytes 47685888 | tf_op jit(solution)/shard_map/nwzkq,wzh->nhkq/dot_general | solution.py:255
  183.5 30.0 %fusion.115 = (f32[15,33,64,64]{3,1,2,0:T(8,128)}, f32[15,33,64,64]{3,1,2,0:T(8,128)}) fusion(f32[15,33,64,128]{3,1,2,0:T(8,128)} %fusion.26), kind=kLoop, calls=%fused_computation.191 | loop fusion | bytes 32440320 | tf_op jit(solution)/shard_map/slice | solution.py:262
  214.2 7.2 %all_gather.3 = bf16[4,32,1024]{2,1,0:T(8,128)(2,1)S(1)} all-gather(bf16[1,32,1024]{2,1,0:T(8,128)(2,1)S(1)} %copy-done.1), channel_id=1, replica_groups=mesh['vol'=8,'orient'=4] {'orient'}, dimensions={0}, use_global_device_ids=true | all-gather | bytes 327680 | tf_op jit(solution)/shard_map/all_gather | solution.py:300
  221.8 2.0 reshape.877
  224.0 2.4 convert_bitcast_fusion
  226.3 6.8 %copy.27 = bf16[4,2,32,32,64]{3,2,1,4,0:T(8,128)(2,1)} copy(bf16[4,2,32,32,64]{4,3,2,0,1:T(8,128)(2,1)S(1)} %convert_bitcast_fusion) | data formatting | bytes 2097152 | tf_op jit(solution)/shard_map/convert_element_type | solution.py:36
  233.3 5.5 %fusion.30 = bf16[4,2,32,64,64]{3,2,4,0,1:T(8,128)(2,1)} fusion(bf16[4,2,32,32,64]{3,2,1,4,0:T(8,128)(2,1)} %copy.27, bf16[1,32,2,64]{3,1,2,0:T(8,128)(2,1)S(1)} %get-tuple-element.114, bf16[1,32,2,64]{3,1,2,0:T(8,128)(2,1)S(1)} %get-tuple-element.113), kind=kOutput, calls=%fused_computation.31 | convolution fusion | flops 135274496 | bytes 3162112 | tf_op jit(solution)/shard_map/ncayk,cydj->ndajk/dot_general | solution.py:48
  238.8 10.9 %copy.28 = bf16[4,2,32,64,64]{4,2,1,3,0:T(8,128)(2,1)} copy(bf16[4,2,32,64,64]{3,2,4,0,1:T(8,128)(2,1)} %fusion.30) | data formatting | bytes 4194304 | tf_op jit(solution)/shard_map/convert_element_type | solution.py:36
  249.9 6.1 %fusion.29 = bf16[4,33,64,2,64]{2,1,4,0,3:T(8,128)(2,1)} fusion(bf16[4,2,32,64,64]{4,2,1,3,0:T(8,128)(2,1)} %copy.28, bf16[1,32,2,33]{3,1,0,2:T(8,128)(2,1)S(1)} %get-tuple-element.112, bf16[1,32,2,33]{3,1,0,2:T(8,128)(2,1)S(1)} %get-tuple-element.111), kind=kOutput, calls=%fused_computation.30 | convolution fusion | flops 139510272 | bytes 4268288 | tf_op jit(solution)/shard_map/ncajk,cadh->ndhjk/dot_general | solution.py:48
  255.9 15.1 %copy.48 = bf16[4,33,64,2,64]{4,3,1,2,0:T(2,128)(2,1)} copy(bf16[4,33,64,2,64]{2,1,4,0,3:T(8,128)(2,1)} %fusion.29) | data formatting | bytes 4325376 | tf_op jit(solution)/shard_map/while | solution.py:290
  271.0 8.6 %reshape.893 = bf16[4,33,64,128]{3,1,2,0:T(8,128)(2,1)} reshape(bf16[4,33,64,2,64]{4,3,1,2,0:T(2,128)(2,1)} %copy.48) | data formatting | bytes 4325376 | tf_op jit(solution)/shard_map/while | solution.py:290
  280.4 256.1 %while.11 = (s32[]{:T(128)}, f32[4,15]{1,0:T(4,128)S(1)}, bf16[4,33,64,128]{3,1,2,0:T(8,128)(2,1)}, f32[15,33,64,64]{3,1,2,0:T(8,128)}, f32[15,33,64,64]{3,1,2,0...) while((s32[]{:T(128)}, f32[4,15]{1,0:T(4,128)S(1)}, ...), condition=%wide.region_5.6_spmd.clone, body=%wide.region_3.5_spmd.sunk.clone | while | flops 223382000 | bytes 157521328 | solution.py:290
  280.7 1.1 dynamic-slice_bitcast_fusion.3
  282.2 23.2 %fusion.142 = (bf16[15,33,64,64]{3,1,2,0:T(8,128)(2,1)}, bf16[15,33,64,64]{3,1,2,0:T(8,128)(2,1)}) fusion(f32[15,33,64,64]{3,1,2,0:T(8,128)} %get-tuple-element.246, f32[33,64,64]{2,0,1:T(8,128)S(1)} %get-tuple-element.208, f32[15,33,64,64]{3,1,2,0:T(8,128)} %get-tuple-element.247, f32[33,64,64]{2,0,1:T(8,128)S(1)} %get-tuple-element.209), kind=kLoop, calls=%fused_computation.190.clone.1.clone | loop fusion | flops 10137600 | bytes 25411584 | tf_op jit(solution)/shard_map/while/body/eval_jaxpr/neg | solution.py:281
  305.4 1.1 slice-done.3
  306.5 0.8 slice-done.4
  307.3 12.5 %add_convert_fusion.3 = bf16[15,33,64,64]{3,1,2,0:T(8,128)(2,1)} fusion(f32[15,33,64,64]{3,1,2,0:T(8,128)S(1)} %bitcast.148, f32[15,33,64,64]{3,1,2,0:T(8,128)} %get-tuple-element.246, f32[33,64,64]{2,0,1:T(8,128)S(1)} %get-tuple-element.208, f32[33,64,64]{2,0,1:T(8,128)S(1)} %get-tuple-element.209), kind=kLoop, calls=%fused_computation.5.clone.1.clone | loop fusion | flops 8110080 | bytes 21356544 | tf_op jit(solution)/shard_map/while/body/eval_jaxpr/convert_element_type | solution.py:36
  319.8 18.7 %maximum_bitcast_fusion.14 = (bf16[15,1,33,64,128]{4,2,1,3,0:T(8,128)(2,1)S(1)}, bf16[15,1,33,64,128]{4,2,1,3,0:T(8,128)(2,1)S(1)}) fusion(bf16[15,33,64,64]{3,1,2,0:T(8,128)(2,1)} %get-tuple-element.210, bf16[15,33,64,64]{3,1,2,0:T(8,128)(2,1)} %add_convert_fusion.3, bf16[15,33,64,64]{3,1,2,0:T(8,128)(2,1)} %get-tuple-element.211), kind=kLoop, calls=%fused_computation.6.clone.1.clone | loop fusion | flops 32440320 | bytes 28385280 | tf_op jit(solution)/shard_map/while/body/eval_jaxpr/stack | solution.py:282
  338.6 3.6 fusion.143
  342.2 1.6 fusion.144
  344.6 1.1 dynamic-slice_bitcast_fusion.3
  346.1 23.2 %fusion.142 = (bf16[15,33,64,64]{3,1,2,0:T(8,128)(2,1)}, bf16[15,33,64,64]{3,1,2,0:T(8,128)(2,1)}) fusion(f32[15,33,64,64]{3,1,2,0:T(8,128)} %get-tuple-element.246, f32[33,64,64]{2,0,1:T(8,128)S(1)} %get-tuple-element.208, f32[15,33,64,64]{3,1,2,0:T(8,128)} %get-tuple-element.247, f32[33,64,64]{2,0,1:T(8,128)S(1)} %get-tuple-element.209), kind=kLoop, calls=%fused_computation.190.clone.1.clone | loop fusion | flops 10137600 | bytes 25411584 | tf_op jit(solution)/shard_map/while/body/eval_jaxpr/neg | solution.py:281
  369.4 1.1 slice-done.3
  370.4 0.8 slice-done.4
  371.3 12.5 %add_convert_fusion.3 = bf16[15,33,64,64]{3,1,2,0:T(8,128)(2,1)} fusion(f32[15,33,64,64]{3,1,2,0:T(8,128)S(1)} %bitcast.148, f32[15,33,64,64]{3,1,2,0:T(8,128)} %get-tuple-element.246, f32[33,64,64]{2,0,1:T(8,128)S(1)} %get-tuple-element.208, f32[33,64,64]{2,0,1:T(8,128)S(1)} %get-tuple-element.209), kind=kLoop, calls=%fused_computation.5.clone.1.clone | loop fusion | flops 8110080 | bytes 21356544 | tf_op jit(solution)/shard_map/while/body/eval_jaxpr/convert_element_type | solution.py:36
  383.8 18.7 %maximum_bitcast_fusion.14 = (bf16[15,1,33,64,128]{4,2,1,3,0:T(8,128)(2,1)S(1)}, bf16[15,1,33,64,128]{4,2,1,3,0:T(8,128)(2,1)S(1)}) fusion(bf16[15,33,64,64]{3,1,2,0:T(8,128)(2,1)} %get-tuple-element.210, bf16[15,33,64,64]{3,1,2,0:T(8,128)(2,1)} %add_convert_fusion.3, bf16[15,33,64,64]{3,1,2,0:T(8,128)(2,1)} %get-tuple-element.211), kind=kLoop, calls=%fused_computation.6.clone.1.clone | loop fusion | flops 32440320 | bytes 28385280 | tf_op jit(solution)/shard_map/while/body/eval_jaxpr/stack | solution.py:282
  402.5 3.6 fusion.143
  406.1 1.6 fusion.144
  408.6 1.1 dynamic-slice_bitcast_fusion.3
  410.1 23.2 %fusion.142 = (bf16[15,33,64,64]{3,1,2,0:T(8,128)(2,1)}, bf16[15,33,64,64]{3,1,2,0:T(8,128)(2,1)}) fusion(f32[15,33,64,64]{3,1,2,0:T(8,128)} %get-tuple-element.246, f32[33,64,64]{2,0,1:T(8,128)S(1)} %get-tuple-element.208, f32[15,33,64,64]{3,1,2,0:T(8,128)} %get-tuple-element.247, f32[33,64,64]{2,0,1:T(8,128)S(1)} %get-tuple-element.209), kind=kLoop, calls=%fused_computation.190.clone.1.clone | loop fusion | flops 10137600 | bytes 25411584 | tf_op jit(solution)/shard_map/while/body/eval_jaxpr/neg | solution.py:281
  433.4 1.1 slice-done.3
  435.2 12.5 %add_convert_fusion.3 = bf16[15,33,64,64]{3,1,2,0:T(8,128)(2,1)} fusion(f32[15,33,64,64]{3,1,2,0:T(8,128)S(1)} %bitcast.148, f32[15,33,64,64]{3,1,2,0:T(8,128)} %get-tuple-element.246, f32[33,64,64]{2,0,1:T(8,128)S(1)} %get-tuple-element.208, f32[33,64,64]{2,0,1:T(8,128)S(1)} %get-tuple-element.209), kind=kLoop, calls=%fused_computation.5.clone.1.clone | loop fusion | flops 8110080 | bytes 21356544 | tf_op jit(solution)/shard_map/while/body/eval_jaxpr/convert_element_type | solution.py:36
  447.8 18.7 %maximum_bitcast_fusion.14 = (bf16[15,1,33,64,128]{4,2,1,3,0:T(8,128)(2,1)S(1)}, bf16[15,1,33,64,128]{4,2,1,3,0:T(8,128)(2,1)S(1)}) fusion(bf16[15,33,64,64]{3,1,2,0:T(8,128)(2,1)} %get-tuple-element.210, bf16[15,33,64,64]{3,1,2,0:T(8,128)(2,1)} %add_convert_fusion.3, bf16[15,33,64,64]{3,1,2,0:T(8,128)(2,1)} %get-tuple-element.211), kind=kLoop, calls=%fused_computation.6.clone.1.clone | loop fusion | flops 32440320 | bytes 28385280 | tf_op jit(solution)/shard_map/while/body/eval_jaxpr/stack | solution.py:282
  466.5 3.6 fusion.143
  470.1 1.6 fusion.144
  472.6 1.1 dynamic-slice_bitcast_fusion.3
  474.1 23.2 %fusion.142 = (bf16[15,33,64,64]{3,1,2,0:T(8,128)(2,1)}, bf16[15,33,64,64]{3,1,2,0:T(8,128)(2,1)}) fusion(f32[15,33,64,64]{3,1,2,0:T(8,128)} %get-tuple-element.246, f32[33,64,64]{2,0,1:T(8,128)S(1)} %get-tuple-element.208, f32[15,33,64,64]{3,1,2,0:T(8,128)} %get-tuple-element.247, f32[33,64,64]{2,0,1:T(8,128)S(1)} %get-tuple-element.209), kind=kLoop, calls=%fused_computation.190.clone.1.clone | loop fusion | flops 10137600 | bytes 25411584 | tf_op jit(solution)/shard_map/while/body/eval_jaxpr/neg | solution.py:281
  497.3 1.1 slice-done.3
  499.2 12.5 %add_convert_fusion.3 = bf16[15,33,64,64]{3,1,2,0:T(8,128)(2,1)} fusion(f32[15,33,64,64]{3,1,2,0:T(8,128)S(1)} %bitcast.148, f32[15,33,64,64]{3,1,2,0:T(8,128)} %get-tuple-element.246, f32[33,64,64]{2,0,1:T(8,128)S(1)} %get-tuple-element.208, f32[33,64,64]{2,0,1:T(8,128)S(1)} %get-tuple-element.209), kind=kLoop, calls=%fused_computation.5.clone.1.clone | loop fusion | flops 8110080 | bytes 21356544 | tf_op jit(solution)/shard_map/while/body/eval_jaxpr/convert_element_type | solution.py:36
  511.8 18.7 %maximum_bitcast_fusion.14 = (bf16[15,1,33,64,128]{4,2,1,3,0:T(8,128)(2,1)S(1)}, bf16[15,1,33,64,128]{4,2,1,3,0:T(8,128)(2,1)S(1)}) fusion(bf16[15,33,64,64]{3,1,2,0:T(8,128)(2,1)} %get-tuple-element.210, bf16[15,33,64,64]{3,1,2,0:T(8,128)(2,1)} %add_convert_fusion.3, bf16[15,33,64,64]{3,1,2,0:T(8,128)(2,1)} %get-tuple-element.211), kind=kLoop, calls=%fused_computation.6.clone.1.clone | loop fusion | flops 32440320 | bytes 28385280 | tf_op jit(solution)/shard_map/while/body/eval_jaxpr/stack | solution.py:282
  530.5 3.6 fusion.143
  534.1 1.6 fusion.144
  537.8 1.1 select_reduce_fusion
  (92 shorter events, 14.9 us)
Async XLA Ops:
  16.6 0.7 copy-start
  183.5 30.7 %copy-start.1 = (bf16[1,32,1024]{2,1,0:T(8,128)(2,1)S(1)}, bf16[1,32,1024]{2,1,0:T(8,128)(2,1)}, u32[]{:S(2)}) copy-start(bf16[1,32,1024]{2,1,0:T(8,128)(2,1)} %param.9) | copy-start | bytes 196612
  280.4 256.1 %copy-start.2 = (s32[1,1,8]{2,1,0:T(1,128)S(1)}, s32[1,1,8]{2,1,0:T(1,128)}, u32[]{:S(2)}) copy-start(s32[1,1,8]{2,1,0:T(1,128)} %param.13) | copy-start | bytes 100
  282.1 23.3 %slice-start = ((s8[19660800]{0:T(1024)(128)(4,1)}), s8[4194304]{0:T(1024)(128)(4,1)S(1)}, s32[]{:S(2)}) async-start(s8[19660800]{0:T(1024)(128)(4,1)} %bitcast.147), calls=%async_computation | async-start | bytes 8388608 | tf_op jit(solution)/shard_map/while
  282.1 23.3 %slice-start.1 = ((s8[19660800]{0:T(1024)(128)(4,1)}), s8[4194304]{0:T(1024)(128)(4,1)S(1)}, s32[]{:S(2)}) async-start(s8[19660800]{0:T(1024)(128)(4,1)} %bitcast.147), calls=%async_computation.1 | async-start | bytes 8388608 | tf_op jit(solution)/shard_map/while
  282.1 23.3 %slice-start.2 = ((s8[19660800]{0:T(1024)(128)(4,1)}), s8[4194304]{0:T(1024)(128)(4,1)S(1)}, s32[]{:S(2)}) async-start(s8[19660800]{0:T(1024)(128)(4,1)} %bitcast.147), calls=%async_computation.2 | async-start | bytes 8388608 | tf_op jit(solution)/shard_map/while
  282.1 24.3 %slice-start.3 = ((s8[19660800]{0:T(1024)(128)(4,1)}), s8[4194304]{0:T(1024)(128)(4,1)S(1)}, s32[]{:S(2)}) async-start(s8[19660800]{0:T(1024)(128)(4,1)} %bitcast.147), calls=%async_computation.3 | async-start | bytes 8388608 | tf_op jit(solution)/shard_map/while
  282.1 25.2 %slice-start.4 = ((s8[19660800]{0:T(1024)(128)(4,1)}), s8[2883584]{0:T(1024)(128)(4,1)S(1)}, s32[]{:S(2)}) async-start(s8[19660800]{0:T(1024)(128)(4,1)} %bitcast.147), calls=%async_computation.4 | async-start | bytes 5767168 | tf_op jit(solution)/shard_map/while
  346.1 23.3 %slice-start = ((s8[19660800]{0:T(1024)(128)(4,1)}), s8[4194304]{0:T(1024)(128)(4,1)S(1)}, s32[]{:S(2)}) async-start(s8[19660800]{0:T(1024)(128)(4,1)} %bitcast.147), calls=%async_computation | async-start | bytes 8388608 | tf_op jit(solution)/shard_map/while
  346.1 23.3 %slice-start.1 = ((s8[19660800]{0:T(1024)(128)(4,1)}), s8[4194304]{0:T(1024)(128)(4,1)S(1)}, s32[]{:S(2)}) async-start(s8[19660800]{0:T(1024)(128)(4,1)} %bitcast.147), calls=%async_computation.1 | async-start | bytes 8388608 | tf_op jit(solution)/shard_map/while
  346.1 23.3 %slice-start.2 = ((s8[19660800]{0:T(1024)(128)(4,1)}), s8[4194304]{0:T(1024)(128)(4,1)S(1)}, s32[]{:S(2)}) async-start(s8[19660800]{0:T(1024)(128)(4,1)} %bitcast.147), calls=%async_computation.2 | async-start | bytes 8388608 | tf_op jit(solution)/shard_map/while
  346.1 24.3 %slice-start.3 = ((s8[19660800]{0:T(1024)(128)(4,1)}), s8[4194304]{0:T(1024)(128)(4,1)S(1)}, s32[]{:S(2)}) async-start(s8[19660800]{0:T(1024)(128)(4,1)} %bitcast.147), calls=%async_computation.3 | async-start | bytes 8388608 | tf_op jit(solution)/shard_map/while
  346.1 25.2 %slice-start.4 = ((s8[19660800]{0:T(1024)(128)(4,1)}), s8[2883584]{0:T(1024)(128)(4,1)S(1)}, s32[]{:S(2)}) async-start(s8[19660800]{0:T(1024)(128)(4,1)} %bitcast.147), calls=%async_computation.4 | async-start | bytes 5767168 | tf_op jit(solution)/shard_map/while
  410.0 23.3 %slice-start = ((s8[19660800]{0:T(1024)(128)(4,1)}), s8[4194304]{0:T(1024)(128)(4,1)S(1)}, s32[]{:S(2)}) async-start(s8[19660800]{0:T(1024)(128)(4,1)} %bitcast.147), calls=%async_computation | async-start | bytes 8388608 | tf_op jit(solution)/shard_map/while
  410.1 23.3 %slice-start.1 = ((s8[19660800]{0:T(1024)(128)(4,1)}), s8[4194304]{0:T(1024)(128)(4,1)S(1)}, s32[]{:S(2)}) async-start(s8[19660800]{0:T(1024)(128)(4,1)} %bitcast.147), calls=%async_computation.1 | async-start | bytes 8388608 | tf_op jit(solution)/shard_map/while
  410.1 23.3 %slice-start.2 = ((s8[19660800]{0:T(1024)(128)(4,1)}), s8[4194304]{0:T(1024)(128)(4,1)S(1)}, s32[]{:S(2)}) async-start(s8[19660800]{0:T(1024)(128)(4,1)} %bitcast.147), calls=%async_computation.2 | async-start | bytes 8388608 | tf_op jit(solution)/shard_map/while
  410.1 24.3 %slice-start.3 = ((s8[19660800]{0:T(1024)(128)(4,1)}), s8[4194304]{0:T(1024)(128)(4,1)S(1)}, s32[]{:S(2)}) async-start(s8[19660800]{0:T(1024)(128)(4,1)} %bitcast.147), calls=%async_computation.3 | async-start | bytes 8388608 | tf_op jit(solution)/shard_map/while
  410.1 25.2 %slice-start.4 = ((s8[19660800]{0:T(1024)(128)(4,1)}), s8[2883584]{0:T(1024)(128)(4,1)S(1)}, s32[]{:S(2)}) async-start(s8[19660800]{0:T(1024)(128)(4,1)} %bitcast.147), calls=%async_computation.4 | async-start | bytes 5767168 | tf_op jit(solution)/shard_map/while
  474.0 23.3 %slice-start = ((s8[19660800]{0:T(1024)(128)(4,1)}), s8[4194304]{0:T(1024)(128)(4,1)S(1)}, s32[]{:S(2)}) async-start(s8[19660800]{0:T(1024)(128)(4,1)} %bitcast.147), calls=%async_computation | async-start | bytes 8388608 | tf_op jit(solution)/shard_map/while
  474.0 23.3 %slice-start.1 = ((s8[19660800]{0:T(1024)(128)(4,1)}), s8[4194304]{0:T(1024)(128)(4,1)S(1)}, s32[]{:S(2)}) async-start(s8[19660800]{0:T(1024)(128)(4,1)} %bitcast.147), calls=%async_computation.1 | async-start | bytes 8388608 | tf_op jit(solution)/shard_map/while
  474.0 23.3 %slice-start.2 = ((s8[19660800]{0:T(1024)(128)(4,1)}), s8[4194304]{0:T(1024)(128)(4,1)S(1)}, s32[]{:S(2)}) async-start(s8[19660800]{0:T(1024)(128)(4,1)} %bitcast.147), calls=%async_computation.2 | async-start | bytes 8388608 | tf_op jit(solution)/shard_map/while
  474.0 24.3 %slice-start.3 = ((s8[19660800]{0:T(1024)(128)(4,1)}), s8[4194304]{0:T(1024)(128)(4,1)S(1)}, s32[]{:S(2)}) async-start(s8[19660800]{0:T(1024)(128)(4,1)} %bitcast.147), calls=%async_computation.3 | async-start | bytes 8388608 | tf_op jit(solution)/shard_map/while
  474.1 25.2 %slice-start.4 = ((s8[19660800]{0:T(1024)(128)(4,1)}), s8[2883584]{0:T(1024)(128)(4,1)S(1)}, s32[]{:S(2)}) async-start(s8[19660800]{0:T(1024)(128)(4,1)} %bitcast.147), calls=%async_computation.4 | async-start | bytes 5767168 | tf_op jit(solution)/shard_map/while

commit v5 on v3

--- a/solution.py
+++ b/solution.py
@@ -257,10 +257,10 @@
 
 def match_kj(spectrum_v, box_rms, spectra):
     spectra_kj = jnp.swapaxes(spectra, 3, 4)
-    real_v = spectrum_v[..., :BOX]
-    imag_v = spectrum_v[..., BOX:]
 
     def one(spectrum):
+        real_v = spectrum_v[..., :BOX]
+        imag_v = spectrum_v[..., BOX:]
         real_t = spectrum[0].astype(jnp.float32)[None, None]
         imag_t = spectrum[1].astype(jnp.float32)[None, None]
         rv = real_v[:, None]
@@ -281,7 +281,17 @@
         scores = correlation / (box_rms[:, None] * math.sqrt(float(TMPL**3)))
         return jnp.max(scores, axis=(2, 3, 4))[:, 0]
 
-    values = lax.map(one, spectra_kj)
+    count_r = spectra_kj.shape[0]
+    group = min(4, count_r)
+
+    def one_group(block):
+        return jnp.stack([one(block[i]) for i in range(group)], axis=0)
+
+    blocks = spectra_kj.reshape((count_r // group, group) + spectra_kj.shape[1:])
+    if count_r == group:
+        values = one_group(blocks[0])
+    else:
+        values = lax.map(one_group, blocks).reshape((count_r,) + (spectrum_v.shape[0],))
     return values.T
 
 

time: 378 us -> 354 us (0.937); the launches traced: 378 us -> 349 us
  local copies, waits for them, and re-layouts: 62.3 us -> 40.9 us
  other arithmetic: 91.8 us -> 81.1 us
  matrix products: 81.9 us -> 85.8 us
    convert_element_type x20 -> x7, other arithmetic: 73.3 us -> 0.72 us  [bf(): return x.astype(jnp.bfloat16)]
    another operation x0 -> x2, other arithmetic: none -> 60 us  [one(): cross = jnp.stack([bf(real_p), bf(imag_p)], axis=2)]
    slice x5 -> x0, local copies, waits for them, and re-layouts: 35.7 us -> none  [the longest x1 30 us: match_kj(): imag_v = spectrum_v[..., BOX:]]
    mul x0 -> x9, local copies, waits for them, and re-layouts: none -> 19.6 us  [the longest x8 19.1 us: one(): real_p = real_t * rv + imag_t * iv]
    while x9 -> x0, local copies, waits for them, and re-layouts: 5.13 us -> none
where the time goes in v5:
time: 354 us; the launch traced here: 349 us
  Pallas kernels  133 us (38%)
  matrix products  85.8 us (24%)
  other arithmetic  81.1 us (23%)
  local copies, waits for them, and re-layouts  40.9 us (12%)
  blocking collectives  7.21 us (2%)
    pallas_call x1, Pallas kernels, front(): pl.pallas_call(front_kernel, grid_spec=grid_spec, out_shape=[jax.ShapeDty...  133 us
    another operation x2, other arithmetic, one(): cross = jnp.stack([bf(real_p), bf(imag_p)], axis=2)  60 us
    dot_general x15, matrix products, section(): jnp.einsum(pattern, bf(operand), table, preferred_element_type=jnp.float32)  52.7 us
    dot_general x1, matrix products, box_spectra_of(): jnp.einsum('nwzkq,wzh->nhkq', q2, l3, preferred_element_type=jnp.float32)  33.1 us
    mul x8, local copies, waits for them, and re-layouts, one(): real_p = real_t * rv + imag_t * iv  19.1 us
    convert_element_type x2, local copies, waits for them, and re-layouts, bf(): return x.astype(jnp.bfloat16)  17.9 us
    all_gather x1, blocking collectives, per_device(): all_templates = lax.all_gather(templates, 'orient', axis=0, tiled=True)  7.21 us

profile of v5, /device:TPU:0, one launch (start us, length us, event | category | flops | bytes accessed | tf_op | source)
XLA Modules:
  0.0 349.3 jit_solution(14744138086494982696)
XLA Ops:
  0.6 0.7 iota_subtract_fusion
  1.4 0.7 compare_and_fusion
  2.1 4.2 %fusion.132 = (bf16[15,256,1,64]{1,3,2,0:T(8,128)(2,1)S(1)}, bf16[15,256,1,64]{1,3,2,0:T(8,128)(2,1)S(1)}) fusion(s32[15,256]{1,0:T(8,128)S(1)} %iota_subtract_fusion, pred[15,256]{1,0:T(8,128)(4,1)S(1)} %compare_and_fusion), kind=kLoop, calls=%fused_computation.143 | loop fusion | flops 5160960 | bytes 1002240 | tf_op jit(solution)/shard_map/jit(_where)/select_n | solution.py:82
  6.4 0.8 copy.72.t1_ref
  7.2 0.7 iota_subtract_fusion.1
  7.9 0.7 compare_and_fusion.1
  8.6 4.7 %fusion.135 = (bf16[15,128,64]{2,1,0:T(8,128)(2,1)S(1)}, bf16[15,128,64]{2,1,0:T(8,128)(2,1)S(1)}) fusion(s32[15,128]{1,0:T(8,128)S(1)} %iota_subtract_fusion.1, pred[15,128]{1,0:T(8,128)(4,1)S(1)} %compare_and_fusion.1), kind=kLoop, calls=%fused_computation.146 | loop fusion | flops 2211840 | bytes 501120 | tf_op jit(solution)/shard_map/jit(_where)/select_n | solution.py:212
  13.3 0.3 pad_maximum_fusion.1.l2_ref
  13.6 0.7 broadcast_add_fusion
  14.5 0.3 convert_convert_fusion.bxt_ref
  14.8 0.6 copy-done
  15.5 133.3 %shard_map.77 = (bf16[15,2,64,64,128]{4,3,2,1,0:T(8,128)(2,1)}, f32[15,64,8]{2,1,0:T(8,128)S(1)}) custom-call(s32[15]{0:T(128)S(1)} %bitcast.366, bf16[80,128,256]{2,1,0:T(8,128)(2,1)} %slab_ref.1, bf16[15,256,128]{2,1,0:T(8,128)(2,1)S(1)} %copy.72.t1_ref, bf16[15,128,128]{2,1,0:T(8,128)(2,1)S(1)} %pad_maximum_fusion.1.l2_ref, ...), custom_call_target="tpu_custom_call" | custom-call | tf_op jit(solution)/shard_map/pallas_call | solution.py:239
  148.9 0.5 copy.78
  149.8 33.1 %fusion.22 = f32[15,33,64,128]{3,1,2,0:T(8,128)} fusion(bf16[15,2,64,64,128]{4,3,2,1,0:T(8,128)(2,1)} %get-tuple-element.4, bf16[1,64,33]{1,2,0:T(8,128)(2,1)S(1)} %get-tuple-element.50, bf16[1,64,33]{1,2,0:T(8,128)(2,1)S(1)} %get-tuple-element.51), kind=kOutput, calls=%fused_computation.36 | convolution fusion | flops 1038107136 | bytes 47685888 | tf_op jit(solution)/shard_map/nwzkq,wzh->nhkq/dot_general | solution.py:255
  182.8 7.2 %all_gather.3 = bf16[4,32,1024]{2,1,0:T(8,128)(2,1)S(1)} all-gather(bf16[1,32,1024]{2,1,0:T(8,128)(2,1)S(1)} %copy-done.1), channel_id=1, replica_groups=mesh['vol'=8,'orient'=4] {'orient'}, dimensions={0}, use_global_device_ids=true | all-gather | bytes 327680 | tf_op jit(solution)/shard_map/all_gather | solution.py:304
  190.1 2.0 reshape.1197
  192.2 0.2 multiply_reduce_fusion
  192.7 2.4 convert_bitcast_fusion
  195.0 7.0 %copy.69 = bf16[4,2,32,32,64]{3,2,1,4,0:T(8,128)(2,1)} copy(bf16[4,2,32,32,64]{4,3,2,0,1:T(8,128)(2,1)S(1)} %convert_bitcast_fusion) | data formatting | bytes 2097152 | tf_op jit(solution)/shard_map/convert_element_type | solution.py:36
  202.2 5.6 %fusion.26 = bf16[4,2,32,64,64]{3,2,4,0,1:T(8,128)(2,1)} fusion(bf16[4,2,32,32,64]{3,2,1,4,0:T(8,128)(2,1)} %copy.69, bf16[1,32,2,64]{3,1,2,0:T(8,128)(2,1)S(1)} %get-tuple-element.33, bf16[1,32,2,64]{3,1,2,0:T(8,128)(2,1)S(1)} %get-tuple-element.32), kind=kOutput, calls=%fused_computation.42 | convolution fusion | flops 135274496 | bytes 3162112 | tf_op jit(solution)/shard_map/ncayk,cydj->ndajk/dot_general | solution.py:48
  207.8 10.9 %copy.70 = bf16[4,2,32,64,64]{4,2,1,3,0:T(8,128)(2,1)} copy(bf16[4,2,32,64,64]{3,2,4,0,1:T(8,128)(2,1)} %fusion.26) | data formatting | bytes 4194304 | tf_op jit(solution)/shard_map/convert_element_type | solution.py:36
  218.9 3.7 %fusion.25 = bf16[4,2,33,64,64]{3,2,4,0,1:T(8,128)(2,1)S(1)} fusion(bf16[4,2,32,64,64]{4,2,1,3,0:T(8,128)(2,1)} %copy.70, bf16[1,32,2,33]{3,1,0,2:T(8,128)(2,1)S(1)} %get-tuple-element.31, bf16[1,32,2,33]{3,1,0,2:T(8,128)(2,1)S(1)} %get-tuple-element.30), kind=kOutput, calls=%fused_computation.41 | convolution fusion | flops 139510272 | bytes 4268288 | tf_op jit(solution)/shard_map/ncajk,cadh->ndhjk/dot_general | solution.py:48
  222.6 3.3 fusion.127
  225.9 2.8 copy.92
  228.7 2.8 copy.91
  231.5 19.0 %fusion.20 = (bf16[15,1,1,33,64,64]{5,3,4,0,2,1:T(8,128)(2,1)S(1)}, bf16[15,1,1,33,64,64]{5,3,4,0,2,1:T(8,128)(2,1)}) fusion(f32[15,33,64,128]{3,1,2,0:T(8,128)} %fusion.22, f32[33,64,64]{2,0,1:T(8,128)} %copy.92, f32[33,64,64]{2,0,1:T(8,128)} %copy.91), kind=kLoop, calls=%fused_computation.33 | loop fusion | flops 16220160 | bytes 25411584 | tf_op jit(solution)/shard_map/stack | solution.py:270
  250.5 7.0 %fusion.34 = bf16[15,2,8,64,64]{4,2,3,0,1:T(8,128)(2,1)S(1)} fusion(bf16[1,33,2,8]{1,3,0,2:T(8,128)(2,1)S(1)} %get-tuple-element.39, bf16[1,33,2,8]{1,3,0,2:T(8,128)(2,1)S(1)} %get-tuple-element.38, bf16[15,1,1,33,64,64]{5,3,4,0,2,1:T(8,128)(2,1)} %get-tuple-element.13, bf16[15,1,1,33,64,64]{5,3,4,0,2,1:T(8,128)(2,1)S(1)} %get-tuple-element.12), kind=kOutput, calls=%fused_computation.50 | convolution fusion | flops 134803584 | bytes 10078272 | tf_op jit(solution)/shard_map/nrchkj,chds->nrdskj/dot_general | solution.py:48
  257.8 1.6 fusion.93
  259.7 0.8 fusion.103
  260.4 2.8 copy.74
  263.2 2.8 copy.71
  266.0 2.9 copy.80
  268.9 2.9 copy.79
  271.8 1.5 copy.86
  273.3 0.6 copy.85
  273.9 41.0 %fusion.14 = (bf16[15,1,1,33,64,64]{5,3,4,0,2,1:T(8,128)(2,1)}, bf16[15,1,1,33,64,64]{5,3,4,0,2,1:T(8,128)(2,1)}, bf16[15,1,1,33,64,64]{5,3,4,0,2,1:T(8,128)(2,1...) fusion(f32[15,33,64,128]{3,1,2,0:T(8,128)} %fusion.22, ...), kind=kLoop, calls=%fused_computation.27 | loop fusion | flops 48660480 | bytes 43794432 | tf_op jit(solution)/shard_map/stack | solution.py:270
  314.9 8.6 %fusion.33 = bf16[15,2,8,64,64]{4,2,3,0,1:T(8,128)(2,1)S(1)} fusion(bf16[1,33,2,8]{1,3,0,2:T(8,128)(2,1)S(1)} %get-tuple-element.39, bf16[1,33,2,8]{1,3,0,2:T(8,128)(2,1)S(1)} %get-tuple-element.38, bf16[15,1,1,33,64,64]{5,3,4,0,2,1:T(8,128)(2,1)} %get-tuple-element.16, bf16[15,1,1,33,64,64]{5,3,4,0,2,1:T(8,128)(2,1)} %get-tuple-element.17), kind=kOutput, calls=%fused_computation.49 | convolution fusion | flops 134803584 | bytes 10078272 | tf_op jit(solution)/shard_map/nrchkj,chds->nrdskj/dot_general | solution.py:48
  323.6 1.6 fusion.90
  325.2 0.8 fusion.101
  326.0 9.2 %fusion.32 = bf16[15,2,8,64,64]{4,2,3,0,1:T(8,128)(2,1)S(1)} fusion(bf16[1,33,2,8]{1,3,0,2:T(8,128)(2,1)S(1)} %get-tuple-element.39, bf16[1,33,2,8]{1,3,0,2:T(8,128)(2,1)S(1)} %get-tuple-element.38, bf16[15,1,1,33,64,64]{5,3,4,0,2,1:T(8,128)(2,1)} %get-tuple-element.14, bf16[15,1,1,33,64,64]{5,3,4,0,2,1:T(8,128)(2,1)} %get-tuple-element.15), kind=kOutput, calls=%fused_computation.48 | convolution fusion | flops 134803584 | bytes 10078272 | tf_op jit(solution)/shard_map/nrchkj,chds->nrdskj/dot_general | solution.py:48
  335.3 1.6 fusion.87
  336.9 0.8 fusion.99
  337.7 6.6 %fusion.31 = bf16[15,2,8,64,64]{4,2,3,0,1:T(8,128)(2,1)S(1)} fusion(bf16[1,33,2,8]{1,3,0,2:T(8,128)(2,1)S(1)} %get-tuple-element.39, bf16[1,33,2,8]{1,3,0,2:T(8,128)(2,1)S(1)} %get-tuple-element.38, bf16[15,1,1,33,64,64]{5,3,4,0,2,1:T(8,128)(2,1)} %get-tuple-element.7, bf16[15,1,1,33,64,64]{5,3,4,0,2,1:T(8,128)(2,1)S(1)} %bitcast.368), kind=kOutput, calls=%fused_computation.47 | convolution fusion | flops 134803584 | bytes 10078272 | tf_op jit(solution)/shard_map/nrchkj,chds->nrdskj/dot_general | solution.py:48
  344.3 1.6 fusion.84
  345.9 0.8 fusion.97
  346.7 0.6 reduce_sum.27
  347.4 0.6 iota_compare_fusion.4
  348.0 1.1 fusion.189
  (37 shorter events, 2.0 us)
Async XLA Ops:
  14.8 0.7 copy-start
  149.8 33.1 %copy-start.1 = (bf16[1,32,1024]{2,1,0:T(8,128)(2,1)S(1)}, bf16[1,32,1024]{2,1,0:T(8,128)(2,1)}, u32[]{:S(2)}) copy-start(bf16[1,32,1024]{2,1,0:T(8,128)(2,1)} %param.7) | copy-start | bytes 196612
  325.2 12.5 %slice-start = ((s8[9830400]{0:T(1024)(128)(4,1)}), s8[4194304]{0:T(1024)(128)(4,1)S(1)}, s32[]{:S(2)}) async-start(s8[9830400]{0:T(1024)(128)(4,1)} %bitcast.367), calls=%async_computation | async-start | bytes 8388608
  326.0 11.7 %slice-start.1 = ((s8[9830400]{0:T(1024)(128)(4,1)}), s8[4194304]{0:T(1024)(128)(4,1)S(1)}, s32[]{:S(2)}) async-start(s8[9830400]{0:T(1024)(128)(4,1)} %bitcast.367), calls=%async_computation.1 | async-start | bytes 8388608
  326.0 11.7 %slice-start.2 = ((s8[9830400]{0:T(1024)(128)(4,1)}), s8[1441792]{0:T(1024)(128)(4,1)S(1)}, s32[]{:S(2)}) async-start(s8[9830400]{0:T(1024)(128)(4,1)} %bitcast.367), calls=%async_computation.2 | async-start | bytes 2883584
  337.7 9.0 %copy-start.2 = (s32[1,1,8]{2,1,0:T(1,128)S(1)}, s32[1,1,8]{2,1,0:T(1,128)}, u32[]{:S(2)}) copy-start(s32[1,1,8]{2,1,0:T(1,128)} %param.11) | copy-start | bytes 100
